TPU v7x, 32 devices: a whole 2x2x4 slice. The times are simulated.
32 devices in a mesh: groups: 1, wide: 32 (over z, y, x, core).
Axes of the slice: x: 2, y: 2, z: 4, core: 2. Of those that a mesh axis runs over, the one named last changes fastest.
Arguments:
- trial_bands: bfloat16 [1, 2, 3, 192, 192, 192], P('groups', None, None, 'wide'), may hold values from -160 to 160, as said below
- locked_bands: bfloat16 [4, 2, 3, 192, 192, 192], P('groups', None, None, 'wide'), may hold values from -240 to 240, as said below
- inv_diag: float32 [3, 192, 192, 192], P('groups', None, 'wide'), may hold values from 0.1 to 1
- inv_corr: float32 [3, 192, 192, 192], P('groups', None, 'wide'), may hold values from -0.3 to 0.3
Outputs:
- applied: bfloat16 [1, 2, 3, 192, 192, 192], P('groups', None, None, 'wide')
- rayleigh: float32 [2, 1, 1], P('groups')
Inputs may be any that keep to these rules, and one draw needn't show every extreme that they name: `trial_bands`: sums of locked and independent fields, bounded. `locked_bands`: the locked bands are linearly independent.
All inputs are finite; a program needn't handle non-finite values.
Results may differ from a plain program's by a relative error of at most 0.0013.
Values sent between devices are 32-bit elements; how exact they have to be, the bound alone decides.
No kernel may reach another device: no remote copies, remote signals or barrier semaphores. Data moves between devices by JAX's collectives and lax.ppermute only.
A program may use at most 128 MiB of HBM per device.

v0:
```python
import math

import jax
import jax.numpy as jnp
from jax import lax
from jax.sharding import PartitionSpec as P

highest = lax.Precision.HIGHEST


def signed_wave(indices, length):
    shifted = jnp.where(indices < length // 2, indices, indices - length)
    return shifted.astype(jnp.float32) / (length / 2.0)


def cross_wave(wave_x, wave_y, wave_z, vectors):
    comp_x = vectors[..., 0, :, :, :]
    comp_y = vectors[..., 1, :, :, :]
    comp_z = vectors[..., 2, :, :, :]
    along_x = wave_x[:, None, None]
    along_y = wave_y[None, :, None]
    along_z = wave_z[None, None, :]
    return jnp.stack(
        [
            along_y * comp_z - along_z * comp_y,
            along_z * comp_x - along_x * comp_z,
            along_x * comp_y - along_y * comp_x,
        ],
        axis=-4,
    )


def curl_times_i(waves, stacked):
    wave_x, wave_y, wave_z = waves
    return jnp.stack(
        [
            -cross_wave(wave_x, wave_y, wave_z, stacked[1]),
            cross_wave(wave_x, wave_y, wave_z, stacked[0]),
        ],
        axis=0,
    )


def apply_tensor(vectors, inv_diag, inv_corr):
    coupling_xy = inv_corr[0] * jnp.sqrt(inv_diag[0] * inv_diag[1])
    coupling_xz = inv_corr[1] * jnp.sqrt(inv_diag[0] * inv_diag[2])
    coupling_yz = inv_corr[2] * jnp.sqrt(inv_diag[1] * inv_diag[2])
    comp_x = vectors[..., 0, :, :, :]
    comp_y = vectors[..., 1, :, :, :]
    comp_z = vectors[..., 2, :, :, :]
    out_x = inv_diag[0] * comp_x + coupling_xy * comp_y + coupling_xz * comp_z
    out_y = coupling_xy * comp_x + inv_diag[1] * comp_y + coupling_yz * comp_z
    out_z = coupling_xz * comp_x + coupling_yz * comp_y + inv_diag[2] * comp_z
    return jnp.stack([out_x, out_y, out_z], axis=-4)


def complex_table(length, orient):
    indices = jnp.arange(length, dtype=jnp.int32)
    phases = indices[:, None] * indices[None, :] % length
    angles = phases.astype(jnp.float32) * (2.0 * math.pi / length)
    norm_factor = 1.0 / math.sqrt(length)
    cos_table = jnp.cos(angles) * norm_factor
    sin_table = jnp.sin(angles) * norm_factor * orient
    return jnp.stack(
        [jnp.stack([cos_table, sin_table], axis=0), jnp.stack([-sin_table, cos_table], axis=0)],
        axis=0,
    )


def transform(stacked, axis_dim, orient):
    table = complex_table(stacked.shape[axis_dim + 1], orient)
    if axis_dim == 2:
        return jnp.einsum("pbckyz,pqkn->qbcnyz", stacked, table, precision=highest)
    if axis_dim == 3:
        return jnp.einsum("pbcxkz,pqkn->qbcxnz", stacked, table, precision=highest)
    return jnp.einsum("pbcxyk,pqkn->qbcxyn", stacked, table, precision=highest)


def inner_sum(left_rows, right_rows):
    return jnp.einsum("an,bn->ab", left_rows, right_rows, preferred_element_type=jnp.float32)


def remove_locked(gram_sums, trial_re, trial_im, locked_re, locked_im):
    gram_a, gram_q, proj_re, proj_im = gram_sums
    kept_count = gram_a.shape[0]
    gram = jnp.concatenate(
        [jnp.concatenate([gram_a, gram_q], axis=1), jnp.concatenate([gram_q.T, gram_a], axis=1)],
        axis=0,
    )
    rhs_both = jnp.concatenate([proj_re, proj_im], axis=0)
    lower = jnp.linalg.cholesky(gram)
    middle = lax.linalg.triangular_solve(lower, rhs_both, left_side=True, lower=True)
    coef = lax.linalg.triangular_solve(lower, middle, left_side=True, lower=True, transpose_a=True)
    coef_one = coef[:kept_count]
    coef_two = coef[kept_count:]
    locked_re32 = locked_re.astype(jnp.float32)
    locked_im32 = locked_im.astype(jnp.float32)
    out_re = (
        trial_re.astype(jnp.float32)
        - jnp.einsum("ab,an->bn", coef_one, locked_re32, precision=highest)
        + jnp.einsum("ab,an->bn", coef_two, locked_im32, precision=highest)
    )
    out_im = (
        trial_im.astype(jnp.float32)
        - jnp.einsum("ab,an->bn", coef_one, locked_im32, precision=highest)
        - jnp.einsum("ab,an->bn", coef_two, locked_re32, precision=highest)
    )
    return (out_re, out_im)


def maxwell_pass(spectrum, waves, inv_diag, inv_corr, to_space_fn, to_spectrum_fn):
    curled = curl_times_i(waves, spectrum)
    curled = transform(curled, 4, 1.0)
    curled = transform(curled, 3, 1.0)
    moved = to_space_fn(curled)
    space = transform(moved, 2, 1.0)
    weighted = apply_tensor(space, inv_diag, inv_corr)
    front = transform(weighted, 2, -1.0)
    home = to_spectrum_fn(front)
    home = transform(home, 3, -1.0)
    home = transform(home, 4, -1.0)
    return (curl_times_i(waves, home), space, weighted)


def per_device(trial_bands, locked_bands, inv_diag, inv_corr):
    band_count = trial_bands.shape[0]
    kept_count = locked_bands.shape[0]
    local_x = trial_bands.shape[3]
    grid_len = trial_bands.shape[4]
    trial_re = trial_bands[:, 0].reshape(band_count, -1)
    trial_im = trial_bands[:, 1].reshape(band_count, -1)
    locked_re = locked_bands[:, 0].reshape(kept_count, -1)
    locked_im = locked_bands[:, 1].reshape(kept_count, -1)
    gram_a = inner_sum(locked_re, locked_re) + inner_sum(locked_im, locked_im)
    gram_q = inner_sum(locked_im, locked_re) - inner_sum(locked_re, locked_im)
    proj_re = inner_sum(locked_re, trial_re) + inner_sum(locked_im, trial_im)
    proj_im = inner_sum(locked_re, trial_im) - inner_sum(locked_im, trial_re)
    gram_sums = lax.psum((gram_a, gram_q, proj_re, proj_im), "wide")
    flat_re, flat_im = remove_locked(gram_sums, trial_re, trial_im, locked_re, locked_im)
    shape_local = (band_count, 3, local_x, grid_len, grid_len)
    spectrum = jnp.stack([flat_re.reshape(shape_local), flat_im.reshape(shape_local)], axis=0)
    start_x = lax.axis_index("wide") * local_x
    full_axis = jnp.arange(grid_len, dtype=jnp.int32)
    wave_x = signed_wave(start_x + jnp.arange(local_x, dtype=jnp.int32), grid_len)
    wave_full = signed_wave(full_axis, grid_len)
    waves = (wave_x, wave_full, wave_full)

    def send_out_one(field):
        return lax.all_to_all(field, "wide", split_axis=4, concat_axis=3, tiled=True)

    def send_home_one(field):
        return lax.all_to_all(field, "wide", split_axis=3, concat_axis=4, tiled=True)

    results = [maxwell_pass(spectrum, waves, inv_diag, inv_corr, send_out_one, send_home_one)]
    applied_st, space, weighted = [
        jnp.concatenate([entry[slot] for entry in results], axis=1) for slot in range(3)
    ]
    applied = jnp.stack([applied_st[0], applied_st[1]], axis=1).astype(jnp.bfloat16)
    scale_all = 1.0 / float(grid_len * grid_len * grid_len)
    left_re = space[0].reshape(band_count, -1)
    left_im = space[1].reshape(band_count, -1)
    right_re = weighted[0].reshape(band_count, -1)
    right_im = weighted[1].reshape(band_count, -1)
    part_re = jnp.einsum("an,bn->ab", left_re, right_re, precision=highest) + jnp.einsum(
        "an,bn->ab", left_im, right_im, precision=highest
    )
    part_im = jnp.einsum("an,bn->ab", left_re, right_im, precision=highest) - jnp.einsum(
        "an,bn->ab", left_im, right_re, precision=highest
    )
    total_re, total_im = lax.psum((part_re, part_im), "wide")
    rayleigh = jnp.stack([total_re * scale_all, total_im * scale_all], axis=0)
    return (applied, rayleigh)


def solution(mesh):
    in_specs = (
        P("groups", None, None, "wide", None, None),
        P("groups", None, None, "wide", None, None),
        P("groups", None, "wide", None),
        P("groups", None, "wide", None),
    )
    out_specs = (P("groups", None, None, "wide", None, None), P("groups", None, None))
    return jax.shard_map(
        per_device, mesh=mesh, in_specs=in_specs, out_specs=out_specs, check_vma=False
    )
```

profile of v0, /device:TPU:0, one launch (start us, length us, event | category | flops | bytes accessed | tf_op | source)
XLA Modules:
  0.0 763.4 jit_solution(15540134172055891031)
XLA Ops:
  0.6 10.4 %fusion.89 = (bf16[4,1,3,6,192,192]{5,4,3,2,1,0:T(8,128)(2,1)}, bf16[4,1,3,6,192,192]{5,4,3,2,1,0:T(8,128)(2,1)}) fusion(bf16[4,2,3,6,192,192]{5,4,3,2,1,0:T(8,128)(2,1)} %param.5), kind=kLoop, calls=%fused_computation.148 | loop fusion | bytes 21233664 | tf_op jit(solution)/shard_map/slice | solution.py:132
  11.0 13.4 %reshape.684 = bf16[2654208]{0:T(1024)(128)(2,1)} reshape(bf16[4,1,3,6,192,192]{5,4,3,2,1,0:T(8,128)(2,1)} %get-tuple-element.13) | data formatting | bytes 10616832
  24.4 21.1 %fusion.39 = f32[4,4]{0,1:T(4,128)S(1)} fusion(bf16[4,1,3,6,192,192]{5,4,3,2,1,0:T(8,128)(2,1)} %get-tuple-element.13), kind=kOutput, calls=%fused_computation.71 | convolution fusion | flops 21233664 | bytes 5308480 | tf_op jit(solution)/shard_map/an,bn->ab/dot_general | solution.py:80
  45.5 13.8 %fusion.41 = f32[4,4]{0,1:T(4,128)S(1)} fusion(bf16[4,1,3,6,192,192]{5,4,3,2,1,0:T(8,128)(2,1)S(1)} %bitcast.309, bf16[4,1,3,6,192,192]{5,4,3,2,1,0:T(8,128)(2,1)} %get-tuple-element.13), kind=kOutput, calls=%fused_computation.73 | convolution fusion | flops 21233664 | bytes 10616896 | tf_op jit(solution)/shard_map/an,bn->ab/dot_general | solution.py:80
  59.3 13.3 %reshape.688 = bf16[2654208]{0:T(1024)(128)(2,1)} reshape(bf16[4,1,3,6,192,192]{5,4,3,2,1,0:T(8,128)(2,1)} %get-tuple-element.12) | data formatting | bytes 10616832
  72.7 6.9 reshape_squeeze.16
  79.6 21.3 %fusion.43 = f32[4,4]{0,1:T(4,128)S(1)} fusion(f32[4,4]{0,1:T(4,128)S(1)} %fusion.39, bf16[4,1,3,6,192,192]{5,4,3,2,1,0:T(8,128)(2,1)} %get-tuple-element.12), kind=kOutput, calls=%fused_computation.75 | convolution fusion | flops 21233680 | bytes 5308544 | tf_op jit(solution)/shard_map/an,bn->ab/dot_general | solution.py:80
  101.0 14.4 %fusion.44 = f32[4,4]{0,1:T(4,128)S(1)} fusion(f32[4,4]{0,1:T(4,128)S(1)} %fusion.41, bf16[4,1,3,6,192,192]{5,4,3,2,1,0:T(8,128)(2,1)} %get-tuple-element.13, bf16[4,1,3,6,192,192]{5,4,3,2,1,0:T(8,128)(2,1)S(1)} %bitcast.311), kind=kOutput, calls=%fused_computation.76 | convolution fusion | flops 21233680 | bytes 10616960 | tf_op jit(solution)/shard_map/an,bn->ab/dot_general | solution.py:80
  115.8 3.2 reshape.686
  119.0 6.8 reshape_squeeze.7
  125.8 2.1 reshape.690
  127.9 7.8 %convolution_bitcast_fusion = f32[4]{0:T(128)S(1)} fusion(bf16[4,663552]{1,0:T(4,128)(2,1)} %reshape_squeeze.16, bf16[663552]{0:T(1024)(128)(2,1)} %reshape.686), kind=kOutput, calls=%fused_computation.77 | convolution fusion | flops 5308416 | bytes 6635536 | tf_op jit(solution)/shard_map/an,bn->ab/dot_general | solution.py:80
  135.8 7.4 convolution_bitcast_fusion.2
  143.2 5.9 fusion.48
  149.1 5.9 fusion.46
  155.0 42.2 %all-reduce.1 = (f32[4,4]{0,1:T(4,128)S(1)}, f32[4,4]{0,1:T(4,128)S(1)}, f32[4,1]{0,1:T(1,128)S(1)}, f32[4,1]{0,1:T(1,128)S(1)}) all-reduce(f32[4,4]{0,1:T(4,128)S(1)} %fusion.43, f32[4,4]{0,1:T(4,128)S(1)} %fusion.44, f32[4,1]{0,1:T(1,128)S(1)} %fusion.48, f32[4,1]{0,1:T(1,128)S(1)} %fusion.46), channel_id=1, replica_groups=mesh['groups'=1,'wide'=32] {'wide'}, use_global_device_ids=true, to_apply=%region_0.0 | all-reduce | flops 40 | bytes 320 | tf_op jit(solution)/shard_map/psum | solution.py:138
  200.6 10.5 %fusion.82 = f32[1,663552]{1,0:T(1,128)S(1)} fusion(bf16[4,663552]{1,0:T(4,128)(2,1)} %reshape_squeeze.16, f32[8]{0:T(128)S(1)} %convolution_bitcast_fusion.4), kind=kOutput, calls=%fused_computation.141 | convolution fusion | flops 31850496 | bytes 7962656 | tf_op jit(solution)/shard_map/ab,an->bn/dot_general | solution.py:101
  211.1 10.5 %fusion.80 = f32[1,663552]{1,0:T(1,128)S(1)} fusion(bf16[4,663552]{1,0:T(4,128)(2,1)} %reshape_squeeze.7, f32[8]{0:T(128)S(1)} %convolution_bitcast_fusion.4), kind=kOutput, calls=%fused_computation.139 | convolution fusion | flops 31850496 | bytes 7962656 | tf_op jit(solution)/shard_map/ab,an->bn/dot_general | solution.py:100
  221.7 11.7 %fusion.83 = f32[1,663552]{1,0:T(1,128)} fusion(bf16[4,663552]{1,0:T(4,128)(2,1)} %reshape_squeeze.7, f32[8]{0:T(128)S(1)} %convolution_bitcast_fusion.4), kind=kOutput, calls=%fused_computation.142 | convolution fusion | flops 31850496 | bytes 7962656 | tf_op jit(solution)/shard_map/ab,an->bn/dot_general | solution.py:106
  233.4 9.7 %fusion.81 = f32[1,663552]{1,0:T(1,128)} fusion(bf16[4,663552]{1,0:T(4,128)(2,1)S(1)} %bitcast.315, f32[8]{0:T(128)S(1)} %convolution_bitcast_fusion.4), kind=kOutput, calls=%fused_computation.140 | convolution fusion | flops 31850496 | bytes 7962656 | tf_op jit(solution)/shard_map/ab,an->bn/dot_general | solution.py:105
  243.0 1.6 cosine_multiply_fusion
  244.6 1.5 fusion.65
  247.6 1.8 subtract_add_fusion
  249.4 2.9 squeeze_stack_reshape.7
  252.3 4.8 subtract_subtract_fusion
  257.1 4.9 squeeze_stack_reshape.6
  262.0 3.0 multiply_subtract_fusion.4
  267.5 12.0 %fusion = f32[2,192,3,6,192,1]{4,1,5,3,2,0:T(8,128)S(1)} fusion(f32[1,1,3,6,192,192]{5,4,0,3,2,1:T(8,128)S(1)} %maximum_bitcast_fusion.2, f32[1,1,3,6,192,192]{5,4,0,3,2,1:T(8,128)S(1)} %fusion.21, f32[1,2,192,192]{2,3,0,1:T(8,128)S(1)} %get-tuple-element.42, f32[1,2,192,192]{2,3,0,1:T(8,128)S(1)} %get-tuple-element.43), kind=kOutput, calls=%fused_computation.1 | convolution fusion | flops 6116769792 | bytes 11206656 | tf_op jit(solution)/shard_map/pbcxyk,pqkn->qbcxyn/dot_general | solution.py:76
  279.6 13.5 %fusion.23 = f32[2,1,3,6,192,192]{5,4,3,2,0,1:T(8,128)} fusion(f32[2,192,3,6,192,1]{4,1,5,3,2,0:T(8,128)S(1)} %fusion, f32[1,2,192,192]{2,3,0,1:T(8,128)S(1)} %get-tuple-element.42, f32[1,2,192,192]{2,3,0,1:T(8,128)S(1)} %get-tuple-element.43), kind=kOutput, calls=%fused_computation.41 | convolution fusion | flops 6115442688 | bytes 11206656 | tf_op jit(solution)/shard_map/pbcxkz,pqkn->qbcxnz/dot_general | solution.py:75
  293.1 11.4 %copy.97 = f32[2,1,3,6,192,192]{5,0,3,2,1,4:T(2,128)} copy(f32[2,1,3,6,192,192]{5,4,3,2,0,1:T(8,128)} %fusion.23) | data formatting | bytes 10616832 | tf_op jit(solution)/shard_map/pbcxkz,pqkn->qbcxnz/transpose | solution.py:75
  304.5 4.9 all-to-all-start
  309.4 1.9 slice_bitcast_fusion.8
  312.7 2.4 bitcast_multiply_fusion.2
  315.1 151.6 %all-to-all-done = f32[2,1,3,6,192,192]{5,0,3,2,1,4:T(2,128)} async-done(((f32[2,1,3,6,192,192]{5,0,3,2,1,4:T(2,128)}), f32[2,1,3,6,192,192]{5,0,3,2,1,4:T(2,128)}, u32[]{:S(2)}, u32[]{:S(2)}) %all-to-all-start) | async-done | bytes 5308448 | tf_op jit(solution)/shard_map/all_to_all | solution.py:149
  466.7 9.8 %copy.98 = f32[2,1,3,6,192,192]{5,0,4,3,2,1:T(2,128)} copy(f32[2,1,3,6,192,192]{5,0,3,2,1,4:T(2,128)} %all-to-all-done) | data formatting | bytes 10616832 | tf_op jit(solution)/shard_map/all_to_all | solution.py:149
  476.5 8.6 %copy.99 = f32[2,1,3,32,6,6,192]{6,0,5,4,3,2,1:T(2,128)} copy(f32[2,1,3,32,6,6,192]{6,0,5,3,4,2,1:T(2,128)} %bitcast.312) | data formatting | bytes 10616832 | tf_op jit(solution)/shard_map/all_to_all | solution.py:149
  485.1 14.5 %fusion.26 = f32[2,1,3,192,6,192]{5,3,4,2,0,1:T(8,128)S(1)} fusion(f32[2,3,192,6,192]{4,0,3,2,1:T(2,128)} %bitcast.306, f32[1,2,192,192]{2,3,0,1:T(8,128)S(1)} %copy-done.3, f32[1,2,192,192]{2,3,0,1:T(8,128)S(1)} %copy-done.5), kind=kOutput, calls=%fused_computation.42 | convolution fusion | flops 6115442688 | bytes 11206656 | tf_op jit(solution)/shard_map/pbckyz,pqkn->qbcnyz/dot_general | solution.py:73
  502.5 3.4 pad_maximum_fusion
  505.9 13.5 %fusion.29 = f32[2,1,3,192,6,192]{5,3,4,2,0,1:T(8,128)} fusion(f32[2,3,192,6,192]{4,2,3,1,0:T(8,128)S(1)} %get-tuple-element.18, f32[1,2,192,192]{2,3,1,0:T(8,128)S(1)} %copy-done.7, f32[1,2,192,192]{2,3,1,0:T(8,128)S(1)} %copy-done.6), kind=kOutput, calls=%fused_computation.43 | convolution fusion | flops 6115442688 | bytes 11206656 | tf_op jit(solution)/shard_map/pbckyz,pqkn->qbcnyz/dot_general | solution.py:73
  519.4 11.3 %copy.103 = f32[2,1,3,192,6,192]{5,0,4,2,1,3:T(2,128)} copy(f32[2,1,3,192,6,192]{5,3,4,2,0,1:T(8,128)} %fusion.29) | data formatting | bytes 10616832 | tf_op jit(solution)/shard_map/pbckyz,pqkn->qbcnyz/transpose | solution.py:73
  530.7 3.8 all-to-all-start.1
  534.5 6.4 multiply_reduce_fusion.2
  543.6 167.6 %all-reduce = (f32[1,1]{1,0:T(1,128)}, f32[1,1]{1,0:T(1,128)}) all-reduce(f32[1,1]{1,0:T(1,128)} %bitcast.102, f32[1,1]{1,0:T(1,128)} %bitcast.99), channel_id=1, replica_groups=mesh['groups'=1,'wide'=32] {'wide'}, use_global_device_ids=true, to_apply=%region_7.8 | all-reduce | flops 2 | bytes 16 | tf_op jit(solution)/shard_map/psum | solution.py:170
  713.0 8.3 %copy.104 = f32[2,1,3,192,6,192]{5,0,4,3,2,1:T(2,128)} copy(f32[2,1,3,192,6,192]{5,0,4,2,1,3:T(2,128)} %all-to-all-done.1) | data formatting | bytes 10616832 | tf_op jit(solution)/shard_map/all_to_all | solution.py:152
  721.3 9.4 %copy.105 = f32[2,1,3,6,32,6,192]{6,0,5,4,3,2,1:T(2,128)} copy(f32[2,1,3,6,32,6,192]{6,0,5,3,4,2,1:T(2,128)} %bitcast.313) | data formatting | bytes 10616832 | tf_op jit(solution)/shard_map/all_to_all | solution.py:152
  730.7 14.7 %fusion.32 = f32[2,3,6,192,192]{4,3,2,1,0:T(8,128)S(1)} fusion(f32[2,3,6,192,192]{4,0,3,2,1:T(2,128)} %bitcast.307, f32[1,2,192,192]{2,3,1,0:T(8,128)S(1)} %copy-done.7, f32[1,2,192,192]{2,3,1,0:T(8,128)S(1)} %copy-done.6), kind=kOutput, calls=%fused_computation.44 | convolution fusion | flops 6115442688 | bytes 11206656 | tf_op jit(solution)/shard_map/pbcxkz,pqkn->qbcxnz/dot_general | solution.py:75
  745.4 12.4 %fusion.35 = f32[2,1,3,6,192,192]{5,4,3,2,1,0:T(8,128)S(1)} fusion(f32[2,3,6,192,192]{4,3,2,1,0:T(8,128)S(1)} %fusion.32, f32[1,2,192,192]{2,3,1,0:T(8,128)S(1)} %copy-done.7, f32[1,2,192,192]{2,3,1,0:T(8,128)S(1)} %copy-done.6), kind=kOutput, calls=%fused_computation.45 | convolution fusion | flops 6115442688 | bytes 11206656 | tf_op jit(solution)/shard_map/pbcxyk,pqkn->qbcxyn/dot_general | solution.py:76
  760.8 2.5 pad_maximum_fusion.1
  (91 shorter events, 15.5 us)
Async XLA Ops:
  11.0 34.5 %slice-start = ((s8[7077888]{0:T(1024)(128)(4,1)}), s8[2883584]{0:T(1024)(128)(4,1)S(1)}, s32[]{:S(2)}) async-start(s8[7077888]{0:T(1024)(128)(4,1)} %bitcast.308), calls=%async_computation.2 | async-start | bytes 5767168
  24.4 21.1 %slice-start.1 = ((s8[7077888]{0:T(1024)(128)(4,1)}), s8[4194304]{0:T(1024)(128)(4,1)S(1)}, s32[]{:S(2)}) async-start(s8[7077888]{0:T(1024)(128)(4,1)} %bitcast.308), calls=%async_computation.3 | async-start | bytes 8388608
  72.7 28.3 %slice-start.2 = ((s8[7077888]{0:T(1024)(128)(4,1)}), s8[2883584]{0:T(1024)(128)(4,1)S(1)}, s32[]{:S(2)}) async-start(s8[7077888]{0:T(1024)(128)(4,1)} %bitcast.310), calls=%async_computation.4 | async-start | bytes 5767168
  79.6 21.4 %slice-start.3 = ((s8[7077888]{0:T(1024)(128)(4,1)}), s8[4194304]{0:T(1024)(128)(4,1)S(1)}, s32[]{:S(2)}) async-start(s8[7077888]{0:T(1024)(128)(4,1)} %bitcast.310), calls=%async_computation.5 | async-start | bytes 8388608
  101.0 14.4 %copy-start.16 = (bf16[1,2,3,6,192,192]{5,4,3,2,1,0:T(8,128)(2,1)S(1)}, bf16[1,2,3,6,192,192]{5,4,3,2,1,0:T(8,128)(2,1)}, u32[]{:S(2)}) copy-start(bf16[1,2,3,6,192,192]{5,4,3,2,1,0:T(8,128)(2,1)} %param.4) | copy-start | bytes 7962628
  127.9 15.2 %copy-start.8 = (bf16[663552]{0:T(1024)(128)(2,1)}, bf16[663552]{0:T(1024)(128)(2,1)S(1)}, u32[]{:S(2)}) copy-start(bf16[663552]{0:T(1024)(128)(2,1)S(1)} %reshape.690) | copy-start | bytes 3981316
  127.9 15.2 %slice-start.6 = ((s8[5308416]{0:T(1024)(128)(4,1)}), s8[4194304]{0:T(1024)(128)(4,1)S(1)}, s32[]{:S(2)}) async-start(s8[5308416]{0:T(1024)(128)(4,1)} %bitcast.316), calls=%async_computation.8 | async-start | bytes 8388608
  135.8 7.4 slice-start.7
  143.1 6.0 copy-start.9
  211.1 22.3 %slice-start.4 = ((s8[5308416]{0:T(1024)(128)(4,1)}), s8[4194304]{0:T(1024)(128)(4,1)S(1)}, s32[]{:S(2)}) async-start(s8[5308416]{0:T(1024)(128)(4,1)} %bitcast.314), calls=%async_computation.6 | async-start | bytes 8388608
  221.6 11.7 %slice-start.5 = ((s8[5308416]{0:T(1024)(128)(4,1)}), s8[1114112]{0:T(1024)(128)(4,1)S(1)}, s32[]{:S(2)}) async-start(s8[5308416]{0:T(1024)(128)(4,1)} %bitcast.314), calls=%async_computation.7 | async-start | bytes 2228224
  265.3 0.9 copy-start.18
  265.3 1.0 copy-start.19
  265.3 1.1 copy-start.20
  265.3 1.2 copy-start.21
  265.3 1.2 copy-start.22
  267.5 12.0 %copy-start.2 = (f32[1,2,192,192]{2,3,0,1:T(8,128)}, f32[1,2,192,192]{2,3,0,1:T(8,128)S(1)}, u32[]{:S(2)}) copy-start(f32[1,2,192,192]{2,3,0,1:T(8,128)S(1)} %get-tuple-element.42) | copy-start | bytes 884740
  267.5 12.0 %copy-start.4 = (f32[1,2,192,192]{2,3,0,1:T(8,128)}, f32[1,2,192,192]{2,3,0,1:T(8,128)S(1)}, u32[]{:S(2)}) copy-start(f32[1,2,192,192]{2,3,0,1:T(8,128)S(1)} %get-tuple-element.43) | copy-start | bytes 884740
  304.5 4.9 copy-start.1
  304.5 162.3 %all-to-all-start = ((f32[2,1,3,6,192,192]{5,0,3,2,1,4:T(2,128)}), f32[2,1,3,6,192,192]{5,0,3,2,1,4:T(2,128)}, u32[]{:S(2)}, u32[]{:S(2)}) async-start(f32[2,1,3,6,192,192]{5,0,3,2,1,4:T(2,128)} %copy.97), calls=%async_computation | async-start | bytes 14155776 | tf_op jit(solution)/shard_map/all_to_all | solution.py:149
  309.4 3.3 copy-start.17
  476.5 8.6 %copy-start.3 = (f32[1,2,192,192]{2,3,0,1:T(8,128)S(1)}, f32[1,2,192,192]{2,3,0,1:T(8,128)}, u32[]{:S(2)}) copy-start(f32[1,2,192,192]{2,3,0,1:T(8,128)} %copy-done.2) | copy-start | bytes 884740
  476.5 8.6 %copy-start.5 = (f32[1,2,192,192]{2,3,0,1:T(8,128)S(1)}, f32[1,2,192,192]{2,3,0,1:T(8,128)}, u32[]{:S(2)}) copy-start(f32[1,2,192,192]{2,3,0,1:T(8,128)} %copy-done.4) | copy-start | bytes 884740
  485.1 14.5 %copy-start.10 = (f32[192,6,192]{2,0,1:T(8,128)S(1)}, f32[192,6,192]{2,0,1:T(8,128)}, u32[]{:S(2)}) copy-start(f32[192,6,192]{2,0,1:T(8,128)} %get-tuple-element.36) | copy-start | bytes 2654212
  485.1 14.5 %copy-start.11 = (f32[192,6,192]{2,0,1:T(8,128)S(1)}, f32[192,6,192]{2,0,1:T(8,128)}, u32[]{:S(2)}) copy-start(f32[192,6,192]{2,0,1:T(8,128)} %get-tuple-element.37) | copy-start | bytes 2654212
  485.1 14.5 %copy-start.12 = (f32[192,6,192]{2,0,1:T(8,128)S(1)}, f32[192,6,192]{2,0,1:T(8,128)}, u32[]{:S(2)}) copy-start(f32[192,6,192]{2,0,1:T(8,128)} %get-tuple-element.38) | copy-start | bytes 2654212
  485.1 14.5 %copy-start.13 = (f32[192,6,192]{2,0,1:T(8,128)S(1)}, f32[192,6,192]{2,0,1:T(8,128)}, u32[]{:S(2)}) copy-start(f32[192,6,192]{2,0,1:T(8,128)} %get-tuple-element.21) | copy-start | bytes 2654212
  485.1 14.5 %copy-start.14 = (f32[192,6,192]{2,0,1:T(8,128)S(1)}, f32[192,6,192]{2,0,1:T(8,128)}, u32[]{:S(2)}) copy-start(f32[192,6,192]{2,0,1:T(8,128)} %get-tuple-element.22) | copy-start | bytes 2654212
  485.1 14.5 %copy-start.15 = (f32[192,6,192]{2,0,1:T(8,128)S(1)}, f32[192,6,192]{2,0,1:T(8,128)}, u32[]{:S(2)}) copy-start(f32[192,6,192]{2,0,1:T(8,128)} %get-tuple-element.23) | copy-start | bytes 2654212
  499.6 2.9 copy-start
  502.5 3.4 copy-start.6
  502.5 3.4 copy-start.7
  530.7 182.4 %all-to-all-start.1 = ((f32[2,1,3,192,6,192]{5,0,4,2,1,3:T(2,128)}), f32[2,1,3,192,6,192]{5,0,4,2,1,3:T(2,128)}, u32[]{:S(2)}, u32[]{:S(2)}) async-start(f32[2,1,3,192,6,192]{5,0,4,2,1,3:T(2,128)} %copy.103), calls=%async_computation.1 | async-start | bytes 14155776 | tf_op jit(solution)/shard_map/all_to_all | solution.py:152
where the time goes:
time: 773 us; the launch traced here: 763 us
  matrix products  221 us (29%)
  blocking collectives  210 us (27%)
  waiting for transfers between devices  152 us (20%)
  local copies, waits for them, and re-layouts  130 us (17%)
  other arithmetic  37.5 us (5%)
  starting transfers between devices  8.77 us (1%)
    psum x1, blocking collectives, per_device(): total_re, total_im = lax.psum((part_re, part_im), 'wide')  168 us
    all_to_all x1, waiting for transfers between devices, send_out_one(): lax.all_to_all(field, 'wide', split_axis=4, concat_axis=3, tiled=True)  152 us
    dot_general x8, matrix products, inner_sum(): jnp.einsum('an,bn->ab', left_rows, right_rows, preferred_element_type=jnp...  97.7 us
    psum x1, blocking collectives, per_device(): gram_sums = lax.psum((gram_a, gram_q, proj_re, proj_im), 'wide')  42.2 us
    unnamed x66, local copies, waits for them, and re-layouts  35.7 us
    dot_general x2, matrix products, transform(): return jnp.einsum('pbcxkz,pqkn->qbcxnz', stacked, table, precision=highest)  28.2 us
    dot_general x2, matrix products, transform(): return jnp.einsum('pbckyz,pqkn->qbcnyz', stacked, table, precision=highest)  28 us
    dot_general x2, matrix products, transform(): return jnp.einsum('pbcxyk,pqkn->qbcxyn', stacked, table, precision=highest)  24.4 us
  transfers between devices with their start and end apart: 2, of which 1 were waited for; matrix products, arithmetic and copies ran while one was open for 1% of the time, Pallas kernels for 0%

commit v1 on v0

--- a/solution.py
+++ b/solution.py
@@ -6,6 +6,7 @@
 from jax.sharding import PartitionSpec as P
 
 highest = lax.Precision.HIGHEST
+three_pass = lax.Precision.HIGH
 
 
 def signed_wave(indices, length):
@@ -70,10 +71,10 @@
 def transform(stacked, axis_dim, orient):
     table = complex_table(stacked.shape[axis_dim + 1], orient)
     if axis_dim == 2:
-        return jnp.einsum("pbckyz,pqkn->qbcnyz", stacked, table, precision=highest)
+        return jnp.einsum("pbckyz,pqkn->qbcnyz", stacked, table, precision=three_pass)
     if axis_dim == 3:
-        return jnp.einsum("pbcxkz,pqkn->qbcxnz", stacked, table, precision=highest)
-    return jnp.einsum("pbcxyk,pqkn->qbcxyn", stacked, table, precision=highest)
+        return jnp.einsum("pbcxkz,pqkn->qbcxnz", stacked, table, precision=three_pass)
+    return jnp.einsum("pbcxyk,pqkn->qbcxyn", stacked, table, precision=three_pass)
 
 
 def inner_sum(left_rows, right_rows):
@@ -131,11 +132,20 @@
     trial_im = trial_bands[:, 1].reshape(band_count, -1)
     locked_re = locked_bands[:, 0].reshape(kept_count, -1)
     locked_im = locked_bands[:, 1].reshape(kept_count, -1)
-    gram_a = inner_sum(locked_re, locked_re) + inner_sum(locked_im, locked_im)
-    gram_q = inner_sum(locked_im, locked_re) - inner_sum(locked_re, locked_im)
-    proj_re = inner_sum(locked_re, trial_re) + inner_sum(locked_im, trial_im)
-    proj_im = inner_sum(locked_re, trial_im) - inner_sum(locked_im, trial_re)
-    gram_sums = lax.psum((gram_a, gram_q, proj_re, proj_im), "wide")
+    rows = jnp.concatenate(
+        [locked_bands.reshape((2 * kept_count,) + locked_bands.shape[2:]),
+         trial_bands.reshape((2 * band_count,) + trial_bands.shape[2:])],
+        axis=0,
+    )
+    pairs = jnp.einsum("icxyz,jcxyz->ij", rows, rows, preferred_element_type=jnp.float32)
+    pairs = lax.psum(pairs, "wide")
+    lk = pairs[: 2 * kept_count, : 2 * kept_count].reshape(kept_count, 2, kept_count, 2)
+    lt = pairs[: 2 * kept_count, 2 * kept_count :].reshape(kept_count, 2, band_count, 2)
+    gram_a = lk[:, 0, :, 0] + lk[:, 1, :, 1]
+    gram_q = lk[:, 1, :, 0] - lk[:, 0, :, 1]
+    proj_re = lt[:, 0, :, 0] + lt[:, 1, :, 1]
+    proj_im = lt[:, 0, :, 1] - lt[:, 1, :, 0]
+    gram_sums = (gram_a, gram_q, proj_re, proj_im)
     flat_re, flat_im = remove_locked(gram_sums, trial_re, trial_im, locked_re, locked_im)
     shape_local = (band_count, 3, local_x, grid_len, grid_len)
     spectrum = jnp.stack([flat_re.reshape(shape_local), flat_im.reshape(shape_local)], axis=0)

time: 773 us -> 692 us (0.90)
  matrix products: 221 us -> 105 us
  local copies, waits for them, and re-layouts: 130 us -> 157 us
  other arithmetic: 37.5 us -> 47 us
    dot_general x14 -> x7, matrix products: 178 us -> 61.7 us  [the longest x2 17.7 us: transform(): jnp.einsum('pbckyz,pqkn->qbcnyz', stacked, table, precision=three_pass)]
    reshape x0 -> x2, local copies, waits for them, and re-layouts: none -> 14.4 us  [the longest x1 13.6 us: per_device(): locked_bands.reshape((2 * kept_count,) + locked_bands.shape[2:])]
    convert_element_type x0 -> x2, local copies, waits for them, and re-layouts: none -> 8.33 us  [the longest x1 5 us: remove_locked(): trial_re.astype(jnp.float32)]
    unnamed x66 -> x49, local copies, waits for them, and re-layouts: 35.7 us -> 38 us
    transpose x3 -> x2, local copies, waits for them, and re-layouts: 22.8 us -> 22.7 us  [the longest x1 11.4 us: transform(): jnp.einsum('pbcxkz,pqkn->qbcxnz', stacked, table, precision=three_pass)]
  transfers between devices with their start and end apart: 2 -> 2, of which waited for: 1 -> 1; matrix products, arithmetic and copies ran while one was open for 1% -> 2% of each run, Pallas kernels for 0% -> 0%
where the time goes in v1:
time: 692 us; the launch traced here: 684 us
  blocking collectives  210 us (30%)
  local copies, waits for them, and re-layouts  157 us (23%)
  waiting for transfers between devices  152 us (22%)
  matrix products  105 us (15%)
  other arithmetic  47 us (7%)
  starting transfers between devices  8.7 us (1%)
    psum x1, blocking collectives, per_device(): total_re, total_im = lax.psum((part_re, part_im), 'wide')  168 us
    all_to_all x1, waiting for transfers between devices, send_out_one(): lax.all_to_all(field, 'wide', split_axis=4, concat_axis=3, tiled=True)  152 us
    psum x1, blocking collectives, per_device(): pairs = lax.psum(pairs, 'wide')  42.1 us
    unnamed x49, local copies, waits for them, and re-layouts  38 us
    all_to_all x2, local copies, waits for them, and re-layouts, send_out_one(): lax.all_to_all(field, 'wide', split_axis=4, concat_axis=3, tiled=True)  18.4 us
    all_to_all x2, local copies, waits for them, and re-layouts, send_home_one(): lax.all_to_all(field, 'wide', split_axis=3, concat_axis=4, tiled=True)  17.7 us
    dot_general x2, matrix products, transform(): jnp.einsum('pbckyz,pqkn->qbcnyz', stacked, table, precision=three_pass)  17.7 us
    dot_general x2, matrix products, transform(): jnp.einsum('pbcxkz,pqkn->qbcxnz', stacked, table, precision=three_pass)  17.4 us
  transfers between devices with their start and end apart: 2, of which 1 were waited for; matrix products, arithmetic and copies ran while one was open for 2% of the time, Pallas kernels for 0%

profile of v1, /device:TPU:0, one launch (start us, length us, event | category | flops | bytes accessed | tf_op | source)
XLA Modules:
  0.0 684.5 jit_solution(1168826543064035705)
XLA Ops:
  0.6 13.6 %copy.136 = bf16[8,3,6,192,192]{4,0,3,2,1:T(8,128)(2,1)S(1)} copy(bf16[8,3,6,192,192]{4,3,2,1,0:T(8,128)(2,1)} %bitcast.246) | data formatting | bytes 21233664 | tf_op jit(solution)/shard_map/reshape | solution.py:136
  14.3 7.5 %copy.177 = bf16[1,2,3,6,192,192]{5,1,4,3,2,0:T(2,128)(2,1)} copy(bf16[1,2,3,6,192,192]{5,4,3,2,1,0:T(8,128)(2,1)} %param.4) | data formatting | bytes 5308416 | tf_op args[0]
  21.7 14.3 %fusion.39 = f32[10,10]{1,0:T(8,128)S(1)} fusion(bf16[2,3,6,192,192]{4,0,3,2,1:T(2,128)(2,1)} %bitcast.251, bf16[8,3,6,192,192]{4,0,3,2,1:T(8,128)(2,1)S(1)} %copy.136), kind=kOutput, calls=%fused_computation.72 | convolution fusion | flops 159252480 | bytes 13271440 | tf_op jit(solution)/shard_map/icxyz,jcxyz->ij/dot_general | solution.py:140
  36.0 42.1 %psum.21 = f32[10,10]{1,0:T(8,128)S(1)} all-reduce(f32[10,10]{1,0:T(8,128)S(1)} %fusion.39), channel_id=1, replica_groups=mesh['groups'=1,'wide'=32] {'wide'}, use_global_device_ids=true, to_apply=%region_0.0 | all-reduce | flops 100 | bytes 800 | tf_op jit(solution)/shard_map/psum | solution.py:141
  79.4 10.5 %fusion.84 = (bf16[4,1,3,6,192,192]{5,4,3,2,1,0:T(8,128)(2,1)}, bf16[4,1,3,6,192,192]{5,4,3,2,1,0:T(8,128)(2,1)}) fusion(bf16[4,2,3,6,192,192]{5,4,3,2,1,0:T(8,128)(2,1)} %param.5), kind=kLoop, calls=%fused_computation.142 | loop fusion | bytes 21233664 | tf_op jit(solution)/shard_map/slice | solution.py:133
  89.9 2.6 slice_convert_fusion.1
  101.7 13.3 %reshape.707 = bf16[2654208]{0:T(1024)(128)(2,1)} reshape(bf16[4,1,3,6,192,192]{5,4,3,2,1,0:T(8,128)(2,1)} %get-tuple-element.8) | data formatting | bytes 10616832
  115.0 6.8 reshape_squeeze.5
  121.8 11.6 %fusion.77 = f32[1,663552]{1,0:T(1,128)} fusion(bf16[4,663552]{1,0:T(4,128)(2,1)} %reshape_squeeze.5, f32[8]{0:T(128)S(1)} %convolution_bitcast_fusion), kind=kOutput, calls=%fused_computation.135 | convolution fusion | flops 31850496 | bytes 7962656 | tf_op jit(solution)/shard_map/ab,an->bn/dot_general | solution.py:107
  133.4 9.7 %fusion.74 = f32[1,663552]{1,0:T(1,128)} fusion(bf16[4,663552]{1,0:T(4,128)(2,1)S(1)} %copy-done.10, f32[8]{0:T(128)S(1)} %convolution_bitcast_fusion), kind=kOutput, calls=%fused_computation.132 | convolution fusion | flops 31850496 | bytes 7962656 | tf_op jit(solution)/shard_map/ab,an->bn/dot_general | solution.py:101
  143.1 13.5 %reshape.705 = bf16[2654208]{0:T(1024)(128)(2,1)} reshape(bf16[4,1,3,6,192,192]{5,4,3,2,1,0:T(8,128)(2,1)} %get-tuple-element.9) | data formatting | bytes 10616832
  156.6 6.8 reshape_squeeze.4
  163.3 11.3 %fusion.75 = f32[1,663552]{1,0:T(1,128)} fusion(bf16[4,663552]{1,0:T(4,128)(2,1)} %reshape_squeeze.4, f32[8]{0:T(128)S(1)} %convolution_bitcast_fusion), kind=kOutput, calls=%fused_computation.133 | convolution fusion | flops 31850496 | bytes 7962656 | tf_op jit(solution)/shard_map/ab,an->bn/dot_general | solution.py:106
  174.6 10.3 %fusion.76 = f32[1,663552]{1,0:T(1,128)} fusion(bf16[4,663552]{1,0:T(4,128)(2,1)S(1)} %copy-done.9, f32[8]{0:T(128)S(1)} %convolution_bitcast_fusion), kind=kOutput, calls=%fused_computation.134 | convolution fusion | flops 31850496 | bytes 7962656 | tf_op jit(solution)/shard_map/ab,an->bn/dot_general | solution.py:102
  184.9 1.6 cosine_multiply_fusion
  186.5 1.5 fusion.58
  188.1 1.5 fusion.61
  189.6 3.3 reshape.659
  192.9 5.3 subtract_subtract_fusion
  198.2 2.9 squeeze_stack_reshape.6
  201.0 5.0 reshape.660
  206.0 5.3 subtract_add_fusion
  211.3 4.6 squeeze_stack_reshape.7
  216.0 2.9 multiply_subtract_fusion.4
  221.6 6.1 fusion.4
  227.8 8.1 %fusion.23 = f32[2,1,3,6,192,192]{5,4,3,2,0,1:T(8,128)} fusion(f32[2,192,3,6,192,1]{4,1,5,3,2,0:T(8,128)S(1)} %fusion.4, f32[1,2,192,192]{2,3,0,1:T(8,128)S(1)} %get-tuple-element.38, f32[1,2,192,192]{2,3,0,1:T(8,128)S(1)} %get-tuple-element.39), kind=kOutput, calls=%fused_computation.40 | convolution fusion | flops 3057795072 | bytes 11206656 | tf_op jit(solution)/shard_map/pbcxkz,pqkn->qbcxnz/dot_general | solution.py:76
  235.9 11.4 %copy.87 = f32[2,1,3,6,192,192]{5,0,3,2,1,4:T(2,128)} copy(f32[2,1,3,6,192,192]{5,4,3,2,0,1:T(8,128)} %fusion.23) | data formatting | bytes 10616832 | tf_op jit(solution)/shard_map/pbcxkz,pqkn->qbcxnz/transpose | solution.py:76
  247.3 5.1 all-to-all-start
  252.4 1.9 slice_bitcast_fusion.8
  254.2 1.4 copy-done.17
  255.6 2.5 bitcast_multiply_fusion.2
  258.1 151.5 %all-to-all-done = f32[2,1,3,6,192,192]{5,0,3,2,1,4:T(2,128)} async-done(((f32[2,1,3,6,192,192]{5,0,3,2,1,4:T(2,128)}), f32[2,1,3,6,192,192]{5,0,3,2,1,4:T(2,128)}, u32[]{:S(2)}, u32[]{:S(2)}) %all-to-all-start) | async-done | bytes 5308448 | tf_op jit(solution)/shard_map/all_to_all | solution.py:159
  409.7 9.8 %copy.88 = f32[2,1,3,6,192,192]{5,0,4,3,2,1:T(2,128)} copy(f32[2,1,3,6,192,192]{5,0,3,2,1,4:T(2,128)} %all-to-all-done) | data formatting | bytes 10616832 | tf_op jit(solution)/shard_map/all_to_all | solution.py:159
  419.4 8.6 %copy.89 = f32[2,1,3,32,6,6,192]{6,0,5,4,3,2,1:T(2,128)} copy(f32[2,1,3,32,6,6,192]{6,0,5,3,4,2,1:T(2,128)} %bitcast.249) | data formatting | bytes 10616832 | tf_op jit(solution)/shard_map/all_to_all | solution.py:159
  428.1 9.2 %fusion.26 = f32[2,1,3,192,6,192]{5,3,4,2,0,1:T(8,128)S(1)} fusion(f32[2,3,192,6,192]{4,0,3,2,1:T(2,128)} %bitcast.247, f32[1,2,192,192]{2,3,0,1:T(8,128)S(1)} %copy-done.6, f32[1,2,192,192]{2,3,0,1:T(8,128)S(1)} %copy-done.8), kind=kOutput, calls=%fused_computation.41 | convolution fusion | flops 3057795072 | bytes 11206656 | tf_op jit(solution)/shard_map/pbckyz,pqkn->qbcnyz/dot_general | solution.py:74
  437.4 1.5 multiply_add_fusion.2
  438.9 1.4 copy-done
  440.3 3.5 pad_maximum_fusion
  443.8 8.5 %fusion.29 = f32[2,1,3,192,6,192]{5,3,4,2,0,1:T(8,128)} fusion(f32[2,3,192,6,192]{4,2,3,1,0:T(8,128)S(1)} %get-tuple-element.14, f32[1,2,192,192]{2,3,1,0:T(8,128)S(1)} %copy-done.4, f32[1,2,192,192]{2,3,1,0:T(8,128)S(1)} %copy-done.3), kind=kOutput, calls=%fused_computation.42 | convolution fusion | flops 3057795072 | bytes 11206656 | tf_op jit(solution)/shard_map/pbckyz,pqkn->qbcnyz/dot_general | solution.py:74
  452.3 11.3 %copy.93 = f32[2,1,3,192,6,192]{5,0,4,2,1,3:T(2,128)} copy(f32[2,1,3,192,6,192]{5,3,4,2,0,1:T(8,128)} %fusion.29) | data formatting | bytes 10616832 | tf_op jit(solution)/shard_map/pbckyz,pqkn->qbcnyz/transpose | solution.py:74
  463.6 3.6 all-to-all-start.1
  467.2 6.4 multiply_reduce_fusion.2
  476.1 167.7 %all-reduce = (f32[1,1]{1,0:T(1,128)}, f32[1,1]{1,0:T(1,128)}) all-reduce(f32[1,1]{1,0:T(1,128)} %bitcast.95, f32[1,1]{1,0:T(1,128)} %bitcast.92), channel_id=1, replica_groups=mesh['groups'=1,'wide'=32] {'wide'}, use_global_device_ids=true, to_apply=%region_4.5 | all-reduce | flops 2 | bytes 16 | tf_op jit(solution)/shard_map/psum | solution.py:180
  645.7 8.3 %copy.94 = f32[2,1,3,192,6,192]{5,0,4,3,2,1:T(2,128)} copy(f32[2,1,3,192,6,192]{5,0,4,2,1,3:T(2,128)} %all-to-all-done.1) | data formatting | bytes 10616832 | tf_op jit(solution)/shard_map/all_to_all | solution.py:162
  654.1 9.4 %copy.95 = f32[2,1,3,6,32,6,192]{6,0,5,4,3,2,1:T(2,128)} copy(f32[2,1,3,6,32,6,192]{6,0,5,3,4,2,1:T(2,128)} %bitcast.250) | data formatting | bytes 10616832 | tf_op jit(solution)/shard_map/all_to_all | solution.py:162
  663.5 9.2 %fusion.32 = f32[2,3,6,192,192]{4,3,2,1,0:T(8,128)S(1)} fusion(f32[2,3,6,192,192]{4,0,3,2,1:T(2,128)} %bitcast.248, f32[1,2,192,192]{2,3,1,0:T(8,128)S(1)} %copy-done.4, f32[1,2,192,192]{2,3,1,0:T(8,128)S(1)} %copy-done.3), kind=kOutput, calls=%fused_computation.43 | convolution fusion | flops 3057795072 | bytes 11206656 | tf_op jit(solution)/shard_map/pbcxkz,pqkn->qbcxnz/dot_general | solution.py:76
  672.7 6.2 fusion.35
  681.7 2.5 pad_maximum_fusion.1
  (74 shorter events, 16.5 us)
Async XLA Ops:
  79.4 10.5 %copy-start.1 = (bf16[1,2,3,6,192,192]{5,4,3,2,1,0:T(8,128)(2,1)S(1)}, bf16[1,2,3,6,192,192]{5,4,3,2,1,0:T(8,128)(2,1)}, u32[]{:S(2)}) copy-start(bf16[1,2,3,6,192,192]{5,4,3,2,1,0:T(8,128)(2,1)} %param.4) | copy-start | bytes 7962628
  121.8 11.6 %copy-start.10 = (bf16[4,663552]{1,0:T(4,128)(2,1)S(1)}, bf16[4,663552]{1,0:T(4,128)(2,1)}, u32[]{:S(2)}) copy-start(bf16[4,663552]{1,0:T(4,128)(2,1)} %reshape_squeeze.5) | copy-start | bytes 15925252
  163.3 11.3 %copy-start.9 = (bf16[4,663552]{1,0:T(4,128)(2,1)S(1)}, bf16[4,663552]{1,0:T(4,128)(2,1)}, u32[]{:S(2)}) copy-start(bf16[4,663552]{1,0:T(4,128)(2,1)} %reshape_squeeze.4) | copy-start | bytes 15925252
  219.3 0.9 copy-start.18
  219.3 1.0 copy-start.19
  219.3 1.1 copy-start.20
  219.3 1.2 copy-start.21
  219.3 1.2 copy-start.22
  221.6 6.2 copy-start.5
  221.6 6.2 copy-start.7
  247.3 5.1 copy-start.2
  247.3 162.4 %all-to-all-start = ((f32[2,1,3,6,192,192]{5,0,3,2,1,4:T(2,128)}), f32[2,1,3,6,192,192]{5,0,3,2,1,4:T(2,128)}, u32[]{:S(2)}, u32[]{:S(2)}) async-start(f32[2,1,3,6,192,192]{5,0,3,2,1,4:T(2,128)} %copy.87), calls=%async_computation | async-start | bytes 14155776 | tf_op jit(solution)/shard_map/all_to_all | solution.py:159
  252.4 3.3 copy-start.17
  419.4 8.6 %copy-start.6 = (f32[1,2,192,192]{2,3,0,1:T(8,128)S(1)}, f32[1,2,192,192]{2,3,0,1:T(8,128)}, u32[]{:S(2)}) copy-start(f32[1,2,192,192]{2,3,0,1:T(8,128)} %copy-done.5) | copy-start | bytes 884740
  419.4 8.6 %copy-start.8 = (f32[1,2,192,192]{2,3,0,1:T(8,128)S(1)}, f32[1,2,192,192]{2,3,0,1:T(8,128)}, u32[]{:S(2)}) copy-start(f32[1,2,192,192]{2,3,0,1:T(8,128)} %copy-done.7) | copy-start | bytes 884740
  428.1 9.3 %copy-start.11 = (f32[192,6,192]{2,0,1:T(8,128)S(1)}, f32[192,6,192]{2,0,1:T(8,128)}, u32[]{:S(2)}) copy-start(f32[192,6,192]{2,0,1:T(8,128)} %get-tuple-element.32) | copy-start | bytes 2654212
  428.1 9.3 %copy-start.12 = (f32[192,6,192]{2,0,1:T(8,128)S(1)}, f32[192,6,192]{2,0,1:T(8,128)}, u32[]{:S(2)}) copy-start(f32[192,6,192]{2,0,1:T(8,128)} %get-tuple-element.33) | copy-start | bytes 2654212
  428.1 9.3 %copy-start.13 = (f32[192,6,192]{2,0,1:T(8,128)S(1)}, f32[192,6,192]{2,0,1:T(8,128)}, u32[]{:S(2)}) copy-start(f32[192,6,192]{2,0,1:T(8,128)} %get-tuple-element.34) | copy-start | bytes 2654212
  428.1 9.3 %copy-start.14 = (f32[192,6,192]{2,0,1:T(8,128)S(1)}, f32[192,6,192]{2,0,1:T(8,128)}, u32[]{:S(2)}) copy-start(f32[192,6,192]{2,0,1:T(8,128)} %get-tuple-element.17) | copy-start | bytes 2654212
  428.1 9.3 %copy-start.15 = (f32[192,6,192]{2,0,1:T(8,128)S(1)}, f32[192,6,192]{2,0,1:T(8,128)}, u32[]{:S(2)}) copy-start(f32[192,6,192]{2,0,1:T(8,128)} %get-tuple-element.18) | copy-start | bytes 2654212
  428.1 9.3 %copy-start.16 = (f32[192,6,192]{2,0,1:T(8,128)S(1)}, f32[192,6,192]{2,0,1:T(8,128)}, u32[]{:S(2)}) copy-start(f32[192,6,192]{2,0,1:T(8,128)} %get-tuple-element.19) | copy-start | bytes 2654212
  437.4 2.9 copy-start
  440.3 3.5 copy-start.3
  440.3 3.5 copy-start.4
  463.6 182.2 %all-to-all-start.1 = ((f32[2,1,3,192,6,192]{5,0,4,2,1,3:T(2,128)}), f32[2,1,3,192,6,192]{5,0,4,2,1,3:T(2,128)}, u32[]{:S(2)}, u32[]{:S(2)}) async-start(f32[2,1,3,192,6,192]{5,0,4,2,1,3:T(2,128)} %copy.93), calls=%async_computation.1 | async-start | bytes 14155776 | tf_op jit(solution)/shard_map/all_to_all | solution.py:162

commit v2 on v1

--- a/solution.py
+++ b/solution.py
@@ -1,9 +1,14 @@
 import math
+
+import ml_dtypes
+import numpy as np
 
 import jax
 import jax.numpy as jnp
 from jax import lax
 from jax.sharding import PartitionSpec as P
+from jax.experimental import pallas as pl
+from jax.experimental.pallas import tpu as pltpu
 
 highest = lax.Precision.HIGHEST
 three_pass = lax.Precision.HIGH
@@ -77,6 +82,116 @@
     return jnp.einsum("pbcxyk,pqkn->qbcxyn", stacked, table, precision=three_pass)
 
 
+def split_hi_lo(values):
+    scaled = values * 65537.0
+    top = scaled - (scaled - values)
+    return top.astype(jnp.bfloat16), (values - top).astype(jnp.bfloat16)
+
+
+def dot_right(values, table_hi, table_lo):
+    high, low = split_hi_lo(values)
+    f32 = jnp.float32
+    return (
+        jnp.dot(high, table_hi, preferred_element_type=f32)
+        + jnp.dot(low, table_hi, preferred_element_type=f32)
+        + jnp.dot(high, table_lo, preferred_element_type=f32)
+    )
+
+
+def dot_left(table_hi, table_lo, values):
+    high, low = split_hi_lo(values)
+    f32 = jnp.float32
+    return (
+        jnp.dot(table_hi, high, preferred_element_type=f32)
+        + jnp.dot(table_hi, low, preferred_element_type=f32)
+        + jnp.dot(table_lo, high, preferred_element_type=f32)
+    )
+
+
+def front_kernel(coef_ref, qx_ref, trial_ref, locked_ref, chi_ref, clo_ref, shi_ref, slo_ref, out_ref):
+    band = pl.program_id(0)
+    plane = pl.program_id(1)
+    kept = locked_ref.shape[0]
+    size = trial_ref.shape[-1]
+    f32 = jnp.float32
+    first = [coef_ref[band, k] for k in range(kept)]
+    second = [coef_ref[band, kept + k] for k in range(kept)]
+    part_re = []
+    part_im = []
+    for comp in range(3):
+        acc_re = trial_ref[0, 0, comp, 0].astype(f32)
+        acc_im = trial_ref[0, 1, comp, 0].astype(f32)
+        for k in range(kept):
+            l_re = locked_ref[k, 0, comp, 0].astype(f32)
+            l_im = locked_ref[k, 1, comp, 0].astype(f32)
+            acc_re = acc_re - first[k] * l_re + second[k] * l_im
+            acc_im = acc_im - first[k] * l_im - second[k] * l_re
+        part_re.append(acc_re)
+        part_im.append(acc_im)
+    rows = lax.broadcasted_iota(jnp.int32, (size, 1), 0)
+    cols = lax.broadcasted_iota(jnp.int32, (1, size), 1)
+    half = size // 2
+    wave_y = jnp.where(rows < half, rows, rows - size).astype(f32) / (size / 2.0)
+    wave_z = jnp.where(cols < half, cols, cols - size).astype(f32) / (size / 2.0)
+    waves = (qx_ref[plane], wave_y, wave_z)
+    c_hi = chi_ref[...]
+    c_lo = clo_ref[...]
+    s_hi = shi_ref[...]
+    s_lo = slo_ref[...]
+    for comp in range(3):
+        a = (comp + 1) % 3
+        b = (comp + 2) % 3
+        cur_re = -(waves[a] * part_im[b] - waves[b] * part_im[a])
+        cur_im = waves[a] * part_re[b] - waves[b] * part_re[a]
+        z_re = dot_right(cur_re, c_hi, c_lo) - dot_right(cur_im, s_hi, s_lo)
+        z_im = dot_right(cur_re, s_hi, s_lo) + dot_right(cur_im, c_hi, c_lo)
+        y_re = dot_left(c_hi, c_lo, z_re) - dot_left(s_hi, s_lo, z_im)
+        y_im = dot_left(s_hi, s_lo, z_re) + dot_left(c_hi, c_lo, z_im)
+        out_ref[0, 0, comp, 0] = y_re
+        out_ref[1, 0, comp, 0] = y_im
+
+
+def numpy_split(table):
+    full = table.astype(np.float32)
+    high = full.astype(ml_dtypes.bfloat16)
+    low = (full - high.astype(np.float32)).astype(ml_dtypes.bfloat16)
+    return jnp.asarray(high), jnp.asarray(low)
+
+
+def dft_tables(length, orient):
+    indices = np.arange(length, dtype=np.int64)
+    phases = indices[:, None] * indices[None, :] % length
+    angles = phases.astype(np.float64) * (2.0 * math.pi / length)
+    norm_factor = 1.0 / math.sqrt(length)
+    c_hi, c_lo = numpy_split(np.cos(angles) * norm_factor)
+    s_hi, s_lo = numpy_split(np.sin(angles) * norm_factor * orient)
+    return c_hi, c_lo, s_hi, s_lo
+
+
+def front_pass(coef_rows, wave_x, trial_bands, locked_bands):
+    band_count, _, _, local_x, size, _ = trial_bands.shape
+    kept = locked_bands.shape[0]
+    tables = dft_tables(size, 1.0)
+    smem = pl.BlockSpec(memory_space=pltpu.SMEM)
+    table_spec = pl.BlockSpec((size, size), lambda b, x: (0, 0))
+    return pl.pallas_call(
+        front_kernel,
+        grid=(band_count, local_x),
+        in_specs=[
+            smem,
+            smem,
+            pl.BlockSpec((1, 2, 3, 1, size, size), lambda b, x: (b, 0, 0, x, 0, 0)),
+            pl.BlockSpec((kept, 2, 3, 1, size, size), lambda b, x: (0, 0, 0, x, 0, 0)),
+            table_spec,
+            table_spec,
+            table_spec,
+            table_spec,
+        ],
+        out_specs=pl.BlockSpec((2, 1, 3, 1, size, size), lambda b, x: (0, b, 0, x, 0, 0)),
+        out_shape=jax.ShapeDtypeStruct((2, band_count, 3, local_x, size, size), jnp.float32),
+    )(coef_rows, wave_x, trial_bands, locked_bands, *tables)
+
+
 def inner_sum(left_rows, right_rows):
     return jnp.einsum("an,bn->ab", left_rows, right_rows, preferred_element_type=jnp.float32)
 
@@ -109,10 +224,19 @@
     return (out_re, out_im)
 
 
-def maxwell_pass(spectrum, waves, inv_diag, inv_corr, to_space_fn, to_spectrum_fn):
-    curled = curl_times_i(waves, spectrum)
-    curled = transform(curled, 4, 1.0)
-    curled = transform(curled, 3, 1.0)
+def solve_coef(gram_sums):
+    gram_a, gram_q, proj_re, proj_im = gram_sums
+    gram = jnp.concatenate(
+        [jnp.concatenate([gram_a, gram_q], axis=1), jnp.concatenate([gram_q.T, gram_a], axis=1)],
+        axis=0,
+    )
+    rhs_both = jnp.concatenate([proj_re, proj_im], axis=0)
+    lower = jnp.linalg.cholesky(gram)
+    middle = lax.linalg.triangular_solve(lower, rhs_both, left_side=True, lower=True)
+    return lax.linalg.triangular_solve(lower, middle, left_side=True, lower=True, transpose_a=True)
+
+
+def maxwell_pass(curled, waves, inv_diag, inv_corr, to_space_fn, to_spectrum_fn):
     moved = to_space_fn(curled)
     space = transform(moved, 2, 1.0)
     weighted = apply_tensor(space, inv_diag, inv_corr)
@@ -128,10 +252,6 @@
     kept_count = locked_bands.shape[0]
     local_x = trial_bands.shape[3]
     grid_len = trial_bands.shape[4]
-    trial_re = trial_bands[:, 0].reshape(band_count, -1)
-    trial_im = trial_bands[:, 1].reshape(band_count, -1)
-    locked_re = locked_bands[:, 0].reshape(kept_count, -1)
-    locked_im = locked_bands[:, 1].reshape(kept_count, -1)
     rows = jnp.concatenate(
         [locked_bands.reshape((2 * kept_count,) + locked_bands.shape[2:]),
          trial_bands.reshape((2 * band_count,) + trial_bands.shape[2:])],
@@ -146,9 +266,7 @@
     proj_re = lt[:, 0, :, 0] + lt[:, 1, :, 1]
     proj_im = lt[:, 0, :, 1] - lt[:, 1, :, 0]
     gram_sums = (gram_a, gram_q, proj_re, proj_im)
-    flat_re, flat_im = remove_locked(gram_sums, trial_re, trial_im, locked_re, locked_im)
-    shape_local = (band_count, 3, local_x, grid_len, grid_len)
-    spectrum = jnp.stack([flat_re.reshape(shape_local), flat_im.reshape(shape_local)], axis=0)
+    coef = solve_coef(gram_sums)
     start_x = lax.axis_index("wide") * local_x
     full_axis = jnp.arange(grid_len, dtype=jnp.int32)
     wave_x = signed_wave(start_x + jnp.arange(local_x, dtype=jnp.int32), grid_len)
@@ -161,7 +279,8 @@
     def send_home_one(field):
         return lax.all_to_all(field, "wide", split_axis=3, concat_axis=4, tiled=True)
 
-    results = [maxwell_pass(spectrum, waves, inv_diag, inv_corr, send_out_one, send_home_one)]
+    curled = front_pass(coef.T, wave_x, trial_bands, locked_bands)
+    results = [maxwell_pass(curled, waves, inv_diag, inv_corr, send_out_one, send_home_one)]
     applied_st, space, weighted = [
         jnp.concatenate([entry[slot] for entry in results], axis=1) for slot in range(3)
     ]

time: 692 us -> 563 us (0.81)
  local copies, waits for them, and re-layouts: 157 us -> 88.8 us
  matrix products: 105 us -> 48.5 us
  Pallas kernels: 0 us -> 23 us
  other arithmetic: 47 us -> 24.3 us
    dot_general x4 -> x0, matrix products: 42.8 us -> none  [the longest x1 11.6 us: remove_locked(): jnp.einsum('ab,an->bn', coef_two, locked_re32, precision=highest)]
    unnamed x49 -> x18, local copies, waits for them, and re-layouts: 38 us -> 13.9 us
    pallas_call x0 -> x1, Pallas kernels: none -> 23 us  [front_pass(): pl.pallas_call(front_kernel, grid=(band_count, local_x), in_specs=[smem,...]
    another operation x4 -> x0, local copies, waits for them, and re-layouts: 21.1 us -> none  [the longest x1 6.79 us: per_device(): locked_im = locked_bands[:, 1].reshape(kept_count, -1)]
    pallas_call x0 -> x1, local copies, waits for them, and re-layouts: none -> 11.4 us  [front_pass(): pl.pallas_call(front_kernel, grid=(band_count, local_x), in_specs=[smem,...]
    transpose x1 -> x0, local copies, waits for them, and re-layouts: 11.4 us -> none  [transform(): jnp.einsum('pbcxkz,pqkn->qbcxnz', stacked, table, precision=three_pass)]
    slice x1 -> x0, local copies, waits for them, and re-layouts: 10.5 us -> none  [per_device(): locked_re = locked_bands[:, 0].reshape(kept_count, -1)]
    convert_element_type x2 -> x0, local copies, waits for them, and re-layouts: 8.33 us -> none  [the longest x1 5 us: remove_locked(): trial_re.astype(jnp.float32)]
  transfers between devices with their start and end apart: 2 -> 2, of which waited for: 1 -> 1; matrix products, arithmetic and copies ran while one was open for 2% -> 3% of each run, Pallas kernels for 0% -> 0%
where the time goes in v2:
time: 563 us; the launch traced here: 557 us
  blocking collectives  210 us (37%)
  waiting for transfers between devices  149 us (26%)
  local copies, waits for them, and re-layouts  88.8 us (16%)
  matrix products  48.5 us (9%)
  other arithmetic  24.3 us (4%)
  Pallas kernels  23 us (4%)
  starting transfers between devices  8.31 us (1%)
    psum x1, blocking collectives, per_device(): total_re, total_im = lax.psum((part_re, part_im), 'wide')  168 us
    all_to_all x1, waiting for transfers between devices, send_out_one(): lax.all_to_all(field, 'wide', split_axis=4, concat_axis=3, tiled=True)  149 us
    psum x1, blocking collectives, per_device(): pairs = lax.psum(pairs, 'wide')  42.6 us
    pallas_call x1, Pallas kernels, front_pass(): pl.pallas_call(front_kernel, grid=(band_count, local_x), in_specs=[smem,...  23 us
    all_to_all x2, local copies, waits for them, and re-layouts, send_out_one(): lax.all_to_all(field, 'wide', split_axis=4, concat_axis=3, tiled=True)  18.3 us
    dot_general x2, matrix products, transform(): jnp.einsum('pbckyz,pqkn->qbcnyz', stacked, table, precision=three_pass)  18 us
    all_to_all x2, local copies, waits for them, and re-layouts, send_home_one(): lax.all_to_all(field, 'wide', split_axis=3, concat_axis=4, tiled=True)  17.7 us
    dot_general x1, matrix products, per_device(): jnp.einsum('icxyz,jcxyz->ij', rows, rows, preferred_element_type=jnp.floa...  14.3 us
  transfers between devices with their start and end apart: 2, of which 1 were waited for; matrix products, arithmetic and copies ran while one was open for 3% of the time, Pallas kernels for 0%

profile of v2, /device:TPU:0, one launch (start us, length us, event | category | flops | bytes accessed | tf_op | source)
XLA Modules:
  0.0 557.2 jit_solution(536168712261472980)
XLA Ops:
  0.6 13.6 %copy.133 = bf16[8,3,6,192,192]{4,0,3,2,1:T(8,128)(2,1)S(1)} copy(bf16[8,3,6,192,192]{4,3,2,1,0:T(8,128)(2,1)} %bitcast.178) | data formatting | bytes 21233664 | tf_op jit(solution)/shard_map/reshape | solution.py:256
  14.3 7.5 %copy.169 = bf16[1,2,3,6,192,192]{5,1,4,3,2,0:T(2,128)(2,1)} copy(bf16[1,2,3,6,192,192]{5,4,3,2,1,0:T(8,128)(2,1)} %trial_ref.1) | data formatting | bytes 5308416 | tf_op args[0]
  21.7 14.3 %fusion.27 = f32[10,10]{1,0:T(8,128)S(1)} fusion(bf16[2,3,6,192,192]{4,0,3,2,1:T(2,128)(2,1)} %bitcast.185, bf16[8,3,6,192,192]{4,0,3,2,1:T(8,128)(2,1)S(1)} %copy.133), kind=kOutput, calls=%fused_computation.51 | convolution fusion | flops 159252480 | bytes 13271440 | tf_op jit(solution)/shard_map/icxyz,jcxyz->ij/dot_general | solution.py:260
  36.0 42.6 %psum.21 = f32[10,10]{1,0:T(8,128)S(1)} all-reduce(f32[10,10]{1,0:T(8,128)S(1)} %fusion.27), channel_id=1, replica_groups=mesh['groups'=1,'wide'=32] {'wide'}, use_global_device_ids=true, to_apply=%region_0.0 | all-reduce | flops 100 | bytes 800 | tf_op jit(solution)/shard_map/psum | solution.py:261
  78.8 0.1 fusion.49
  79.3 0.7 cholesky.16
  80.1 0.6 compare_reduce_fusion
  80.8 0.6 fusion.50
  81.4 0.6 custom-call.8
  82.1 0.1 add_reduce_fusion
  82.4 0.2 convolution_bitcast_fusion
  82.5 0.7 fusion.52.coef_ref
  83.2 0.6 fusion.58.qx_ref
  83.8 23.0 %shard_map.95 = f32[2,1,3,6,192,192]{5,4,3,2,1,0:T(8,128)} custom-call(f32[1,8]{1,0:T(1,128)} %fusion.52.coef_ref, f32[6]{0:T(128)} %fusion.58.qx_ref, bf16[1,2,3,6,192,192]{5,4,3,2,1,0:T(8,128)(2,1)} %trial_ref.1, bf16[4,2,3,6,192,192]{5,4,3,2,1,0:T(8,128)(2,1)} %locked_ref.1, bf16[192,192]{1,0:T(8,128)(2,1)} %constant.102.clone.chi_ref, ...), custom_call_target="tpu_custom_call" | custom-call | tf_op jit(solution)/shard_map/pallas_call | solution.py:177
  106.8 11.4 %copy.86 = f32[2,1,3,6,192,192]{5,0,3,2,1,4:T(2,128)} copy(f32[2,1,3,6,192,192]{5,4,3,2,1,0:T(8,128)} %shard_map.95) | data formatting | bytes 10616832 | tf_op jit(solution)/shard_map/pallas_call | solution.py:177
  118.2 4.7 all-to-all-start
  122.9 0.8 fusion.48
  123.7 0.8 cosine_multiply_fusion
  124.5 0.8 fusion.45
  125.3 0.9 fusion.37
  126.2 1.2 slice_bitcast_fusion.8
  127.4 1.2 copy-done.6
  128.6 2.5 bitcast_multiply_fusion.2
  131.1 149.2 %all-to-all-done = f32[2,1,3,6,192,192]{5,0,3,2,1,4:T(2,128)} async-done(((f32[2,1,3,6,192,192]{5,0,3,2,1,4:T(2,128)}), f32[2,1,3,6,192,192]{5,0,3,2,1,4:T(2,128)}, u32[]{:S(2)}, u32[]{:S(2)}) %all-to-all-start) | async-done | bytes 5308448 | tf_op jit(solution)/shard_map/all_to_all | solution.py:277
  280.2 9.8 %copy.87 = f32[2,1,3,6,192,192]{5,0,4,3,2,1:T(2,128)} copy(f32[2,1,3,6,192,192]{5,0,3,2,1,4:T(2,128)} %all-to-all-done) | data formatting | bytes 10616832 | tf_op jit(solution)/shard_map/all_to_all | solution.py:277
  290.0 8.6 %copy.88 = f32[2,1,3,32,6,6,192]{6,0,5,4,3,2,1:T(2,128)} copy(f32[2,1,3,32,6,6,192]{6,0,5,3,4,2,1:T(2,128)} %bitcast.183) | data formatting | bytes 10616832 | tf_op jit(solution)/shard_map/all_to_all | solution.py:277
  298.6 9.5 %fusion.17 = f32[2,1,3,192,6,192]{5,3,4,2,0,1:T(8,128)S(1)} fusion(f32[2,3,192,6,192]{4,0,3,2,1:T(2,128)} %bitcast.181, f32[1,2,192,192]{2,3,0,1:T(8,128)S(1)} %get-tuple-element.34, f32[1,2,192,192]{2,3,0,1:T(8,128)} %get-tuple-element.35), kind=kOutput, calls=%fused_computation.31 | convolution fusion | flops 3057795072 | bytes 11206656 | tf_op jit(solution)/shard_map/pbckyz,pqkn->qbcnyz/dot_general | solution.py:79
  308.2 1.6 multiply_add_fusion.2
  309.8 1.2 copy-done
  310.9 3.5 pad_maximum_fusion
  314.5 8.5 %fusion.20 = f32[2,1,3,192,6,192]{5,3,4,2,0,1:T(8,128)} fusion(f32[2,3,192,6,192]{4,2,3,1,0:T(8,128)S(1)} %get-tuple-element.20, f32[1,2,192,192]{2,3,1,0:T(8,128)S(1)} %get-tuple-element.36, f32[1,2,192,192]{2,3,1,0:T(8,128)S(1)} %get-tuple-element.33), kind=kOutput, calls=%fused_computation.32 | convolution fusion | flops 3057795072 | bytes 11206656 | tf_op jit(solution)/shard_map/pbckyz,pqkn->qbcnyz/dot_general | solution.py:79
  323.0 11.4 %copy.92 = f32[2,1,3,192,6,192]{5,0,4,2,1,3:T(2,128)} copy(f32[2,1,3,192,6,192]{5,3,4,2,0,1:T(8,128)} %fusion.20) | data formatting | bytes 10616832 | tf_op jit(solution)/shard_map/pbckyz,pqkn->qbcnyz/transpose | solution.py:79
  334.4 3.6 all-to-all-start.1
  338.0 6.4 %multiply_reduce_fusion.2 = (f32[]{:T(128)}, f32[]{:T(128)}, f32[]{:T(128)}, f32[]{:T(128)}) fusion(f32[2,1,3,192,6,192]{5,3,4,2,0,1:T(8,128)} %copy-done, f32[2,1,3,192,6,192]{5,3,4,2,0,1:T(8,128)} %get-tuple-element.19), kind=kLoop, calls=%fused_computation.28 | loop fusion | flops 5308412 | bytes 10616848 | tf_op jit(solution)/shard_map/an,bn->ab/dot_general | solution.py:293
  347.0 167.7 %all-reduce = (f32[1,1]{1,0:T(1,128)}, f32[1,1]{1,0:T(1,128)}) all-reduce(f32[1,1]{1,0:T(1,128)} %bitcast.71, f32[1,1]{1,0:T(1,128)} %bitcast.68), channel_id=1, replica_groups=mesh['groups'=1,'wide'=32] {'wide'}, use_global_device_ids=true, to_apply=%region_4.5 | all-reduce | flops 2 | bytes 16 | tf_op jit(solution)/shard_map/psum | solution.py:299
  516.0 0.6 pad_maximum_fusion.6
  516.5 8.4 %copy.93 = f32[2,1,3,192,6,192]{5,0,4,3,2,1:T(2,128)} copy(f32[2,1,3,192,6,192]{5,0,4,2,1,3:T(2,128)} %all-to-all-done.1) | data formatting | bytes 10616832 | tf_op jit(solution)/shard_map/all_to_all | solution.py:280
  524.9 9.4 %copy.94 = f32[2,1,3,6,32,6,192]{6,0,5,4,3,2,1:T(2,128)} copy(f32[2,1,3,6,32,6,192]{6,0,5,3,4,2,1:T(2,128)} %bitcast.184) | data formatting | bytes 10616832 | tf_op jit(solution)/shard_map/all_to_all | solution.py:280
  534.3 9.2 %fusion.23 = f32[2,3,6,192,192]{4,3,2,1,0:T(8,128)S(1)} fusion(f32[2,3,6,192,192]{4,0,3,2,1:T(2,128)} %bitcast.182, f32[1,2,192,192]{2,3,1,0:T(8,128)S(1)} %get-tuple-element.36, f32[1,2,192,192]{2,3,1,0:T(8,128)S(1)} %get-tuple-element.33), kind=kOutput, calls=%fused_computation.33 | convolution fusion | flops 3057795072 | bytes 11206656 | tf_op jit(solution)/shard_map/pbcxkz,pqkn->qbcxnz/dot_general | solution.py:81
  543.5 6.1 %fusion.4 = f32[2,192,3,6,192,1]{4,1,5,3,2,0:T(8,128)S(1)} fusion(f32[2,3,6,192,192]{4,3,2,1,0:T(8,128)S(1)} %fusion.23, f32[1,2,192,192]{2,3,1,0:T(8,128)S(1)} %get-tuple-element.36, f32[1,2,192,192]{2,3,1,0:T(8,128)S(1)} %get-tuple-element.33), kind=kOutput, calls=%fused_computation.5 | convolution fusion | flops 3057795072 | bytes 11206656 | tf_op jit(solution)/shard_map/pbcxyk,pqkn->qbcxyn/dot_general | solution.py:82
  549.6 0.3 slice_bitcast_fusion.4
  549.9 0.3 slice_bitcast_fusion.5
  550.2 0.3 copy-done.7
  550.6 1.1 subtract_convert_fusion.1
  551.7 0.5 fusion.26
  552.2 0.4 maximum_bitcast_fusion
  552.6 0.7 pad_maximum_fusion.1
  553.3 3.7 copy.101
  (26 shorter events, 0.9 us)
Async XLA Ops:
  118.2 162.0 %all-to-all-start = ((f32[2,1,3,6,192,192]{5,0,3,2,1,4:T(2,128)}), f32[2,1,3,6,192,192]{5,0,3,2,1,4:T(2,128)}, u32[]{:S(2)}, u32[]{:S(2)}) async-start(f32[2,1,3,6,192,192]{5,0,3,2,1,4:T(2,128)} %copy.86), calls=%async_computation | async-start | bytes 14155776 | tf_op jit(solution)/shard_map/all_to_all | solution.py:277
  122.9 3.3 copy-start.1
  126.2 2.4 copy-start.6
  298.6 9.6 %copy-start.2 = (f32[192,6,192]{2,0,1:T(8,128)S(1)}, f32[192,6,192]{2,0,1:T(8,128)}, u32[]{:S(2)}) copy-start(f32[192,6,192]{2,0,1:T(8,128)} %get-tuple-element.32) | copy-start | bytes 2654212
  298.6 9.6 %copy-start.3 = (f32[192,6,192]{2,0,1:T(8,128)S(1)}, f32[192,6,192]{2,0,1:T(8,128)}, u32[]{:S(2)}) copy-start(f32[192,6,192]{2,0,1:T(8,128)} %get-tuple-element.21) | copy-start | bytes 2654212
  298.6 9.6 %copy-start.4 = (f32[192,6,192]{2,0,1:T(8,128)S(1)}, f32[192,6,192]{2,0,1:T(8,128)}, u32[]{:S(2)}) copy-start(f32[192,6,192]{2,0,1:T(8,128)} %get-tuple-element.22) | copy-start | bytes 2654212
  298.6 9.6 %copy-start.5 = (f32[192,6,192]{2,0,1:T(8,128)S(1)}, f32[192,6,192]{2,0,1:T(8,128)}, u32[]{:S(2)}) copy-start(f32[192,6,192]{2,0,1:T(8,128)} %get-tuple-element.23) | copy-start | bytes 2654212
  308.1 2.8 copy-start
  334.4 182.2 %all-to-all-start.1 = ((f32[2,1,3,192,6,192]{5,0,4,2,1,3:T(2,128)}), f32[2,1,3,192,6,192]{5,0,4,2,1,3:T(2,128)}, u32[]{:S(2)}, u32[]{:S(2)}) async-start(f32[2,1,3,192,6,192]{5,0,4,2,1,3:T(2,128)} %copy.92), calls=%async_computation.1 | async-start | bytes 14155776 | tf_op jit(solution)/shard_map/all_to_all | solution.py:280
  549.9 0.7 copy-start.7

commit v3 on v2

--- a/solution.py
+++ b/solution.py
@@ -1,3 +1,4 @@
+import functools
 import math
 
 import ml_dtypes
@@ -192,6 +193,17 @@
     )(coef_rows, wave_x, trial_bands, locked_bands, *tables)
 
 
+def butterfly_sum(values, axis, count):
+    if count & (count - 1):
+        return lax.psum(values, axis)
+    step = 1
+    while step < count:
+        pairs = [(index, index ^ step) for index in range(count)]
+        values = values + lax.ppermute(values, axis, pairs)
+        step *= 2
+    return values
+
+
 def inner_sum(left_rows, right_rows):
     return jnp.einsum("an,bn->ab", left_rows, right_rows, preferred_element_type=jnp.float32)
 
@@ -247,7 +259,7 @@
     return (curl_times_i(waves, home), space, weighted)
 
 
-def per_device(trial_bands, locked_bands, inv_diag, inv_corr):
+def per_device(wide_count, trial_bands, locked_bands, inv_diag, inv_corr):
     band_count = trial_bands.shape[0]
     kept_count = locked_bands.shape[0]
     local_x = trial_bands.shape[3]
@@ -258,7 +270,7 @@
         axis=0,
     )
     pairs = jnp.einsum("icxyz,jcxyz->ij", rows, rows, preferred_element_type=jnp.float32)
-    pairs = lax.psum(pairs, "wide")
+    pairs = butterfly_sum(pairs, "wide", wide_count)
     lk = pairs[: 2 * kept_count, : 2 * kept_count].reshape(kept_count, 2, kept_count, 2)
     lt = pairs[: 2 * kept_count, 2 * kept_count :].reshape(kept_count, 2, band_count, 2)
     gram_a = lk[:, 0, :, 0] + lk[:, 1, :, 1]
@@ -309,6 +321,7 @@
         P("groups", None, "wide", None),
     )
     out_specs = (P("groups", None, None, "wide", None, None), P("groups", None, None))
+    wide_count = mesh.shape["wide"]
     return jax.shard_map(
-        per_device, mesh=mesh, in_specs=in_specs, out_specs=out_specs, check_vma=False
-    )
+        functools.partial(per_device, wide_count), mesh=mesh, in_specs=in_specs, out_specs=out_specs, check_vma=False
+    )

time: 563 us -> 544 us (0.966)
  blocking collectives: 210 us -> 168 us
  starting transfers between devices: 8.31 us -> 20.4 us
  waiting for transfers between devices: 149 us -> 156 us
    psum x1 -> x0, blocking collectives: 42.6 us -> none  [per_device(): pairs = lax.psum(pairs, 'wide')]
    ppermute x0 -> x5, starting transfers between devices: none -> 10.5 us  [butterfly_sum(): values = values + lax.ppermute(values, axis, pairs)]
    ppermute x0 -> x5, waiting for transfers between devices: none -> 6.76 us  [butterfly_sum(): values = values + lax.ppermute(values, axis, pairs)]
  transfers between devices with their start and end apart: 2 -> 7, of which waited for: 1 -> 6; matrix products, arithmetic and copies ran while one was open for 3% -> 3% of each run, Pallas kernels for 0% -> 0%
where the time goes in v3:
time: 544 us; the launch traced here: 535 us
  blocking collectives  168 us (31%)
  waiting for transfers between devices  156 us (29%)
  local copies, waits for them, and re-layouts  88.8 us (16%)
  matrix products  50 us (9%)
  other arithmetic  24.3 us (4%)
  Pallas kernels  23.1 us (4%)
  starting transfers between devices  20.4 us (4%)
    psum x1, blocking collectives, per_device(): total_re, total_im = lax.psum((part_re, part_im), 'wide')  168 us
    all_to_all x1, waiting for transfers between devices, send_out_one(): lax.all_to_all(field, 'wide', split_axis=4, concat_axis=3, tiled=True)  149 us
    pallas_call x1, Pallas kernels, front_pass(): pl.pallas_call(front_kernel, grid=(band_count, local_x), in_specs=[smem,...  23.1 us
    all_to_all x2, local copies, waits for them, and re-layouts, send_out_one(): lax.all_to_all(field, 'wide', split_axis=4, concat_axis=3, tiled=True)  18.3 us
    dot_general x2, matrix products, transform(): jnp.einsum('pbckyz,pqkn->qbcnyz', stacked, table, precision=three_pass)  18.2 us
    all_to_all x2, local copies, waits for them, and re-layouts, send_home_one(): lax.all_to_all(field, 'wide', split_axis=3, concat_axis=4, tiled=True)  17.7 us
    dot_general x1, matrix products, per_device(): jnp.einsum('icxyz,jcxyz->ij', rows, rows, preferred_element_type=jnp.floa...  15.6 us
    unnamed x18, local copies, waits for them, and re-layouts  13.9 us
  transfers between devices with their start and end apart: 7, of which 6 were waited for; matrix products, arithmetic and copies ran while one was open for 3% of the time, Pallas kernels for 0%

profile of v3, /device:TPU:0, one launch (start us, length us, event | category | flops | bytes accessed | tf_op | source)
XLA Modules:
  0.0 535.3 jit_solution(4248240139334627800)
XLA Ops:
  0.6 13.6 %copy.133 = bf16[8,3,6,192,192]{4,0,3,2,1:T(8,128)(2,1)S(1)} copy(bf16[8,3,6,192,192]{4,3,2,1,0:T(8,128)(2,1)} %bitcast.175) | data formatting | bytes 21233664 | tf_op jit(solution)/shard_map/reshape | solution.py:268
  14.3 7.5 %copy.164 = bf16[1,2,3,6,192,192]{5,1,4,3,2,0:T(2,128)(2,1)} copy(bf16[1,2,3,6,192,192]{5,4,3,2,1,0:T(8,128)(2,1)} %trial_ref.1) | data formatting | bytes 5308416 | tf_op args[0]
  21.7 15.6 %fusion.27 = f32[10,10]{0,1:T(8,128)S(1)} fusion(bf16[2,3,6,192,192]{4,0,3,2,1:T(2,128)(2,1)} %bitcast.182, bf16[8,3,6,192,192]{4,0,3,2,1:T(8,128)(2,1)S(1)} %copy.133), kind=kOutput, calls=%fused_computation.51 | convolution fusion | flops 159252480 | bytes 13271440 | tf_op jit(solution)/shard_map/icxyz,jcxyz->ij/dot_general | solution.py:272
  37.8 0.8 collective-permute-done
  38.7 2.8 collective-permute-start.1
  41.5 1.6 collective-permute-done.1
  43.1 2.0 collective-permute-start.2
  45.2 1.6 collective-permute-done.2
  46.8 2.1 collective-permute-start.3
  48.9 1.6 collective-permute-done.3
  50.5 3.0 collective-permute-start.4
  53.5 0.6 fusion.60.qx_ref
  54.1 1.0 collective-permute-done.4
  55.9 0.7 cholesky.16
  56.7 0.6 compare_reduce_fusion
  57.3 0.6 fusion.50
  58.0 0.6 custom-call.8
  59.1 0.7 fusion.52.coef_ref
  59.8 23.1 %shard_map.95 = f32[2,1,3,6,192,192]{5,4,3,2,1,0:T(8,128)} custom-call(f32[1,8]{1,0:T(1,128)} %fusion.52.coef_ref, f32[6]{0:T(128)} %fusion.60.qx_ref, bf16[1,2,3,6,192,192]{5,4,3,2,1,0:T(8,128)(2,1)} %trial_ref.1, bf16[4,2,3,6,192,192]{5,4,3,2,1,0:T(8,128)(2,1)} %locked_ref.1, bf16[192,192]{1,0:T(8,128)(2,1)} %constant.102.clone.chi_ref, ...), custom_call_target="tpu_custom_call" | custom-call | tf_op jit(solution)/shard_map/pallas_call | solution.py:178
  82.9 11.4 %copy.86 = f32[2,1,3,6,192,192]{5,0,3,2,1,4:T(2,128)} copy(f32[2,1,3,6,192,192]{5,4,3,2,1,0:T(8,128)} %shard_map.95) | data formatting | bytes 10616832 | tf_op jit(solution)/shard_map/pallas_call | solution.py:178
  94.3 6.3 %all-to-all-start = ((f32[2,1,3,6,192,192]{5,0,3,2,1,4:T(2,128)}), f32[2,1,3,6,192,192]{5,0,3,2,1,4:T(2,128)}, u32[]{:S(2)}, u32[]{:S(2)}) async-start(f32[2,1,3,6,192,192]{5,0,3,2,1,4:T(2,128)} %copy.86), calls=%async_computation | async-start | bytes 14155776 | tf_op jit(solution)/shard_map/all_to_all | solution.py:289
  100.7 0.8 fusion.48
  101.4 0.8 cosine_multiply_fusion
  102.3 0.8 fusion.45
  103.0 0.9 fusion.37
  103.9 1.2 slice_bitcast_fusion.8
  105.2 1.2 copy-done.6
  106.4 2.5 bitcast_multiply_fusion.2
  108.8 149.2 %all-to-all-done = f32[2,1,3,6,192,192]{5,0,3,2,1,4:T(2,128)} async-done(((f32[2,1,3,6,192,192]{5,0,3,2,1,4:T(2,128)}), f32[2,1,3,6,192,192]{5,0,3,2,1,4:T(2,128)}, u32[]{:S(2)}, u32[]{:S(2)}) %all-to-all-start) | async-done | bytes 5308448 | tf_op jit(solution)/shard_map/all_to_all | solution.py:289
  258.0 9.8 %copy.87 = f32[2,1,3,6,192,192]{5,0,4,3,2,1:T(2,128)} copy(f32[2,1,3,6,192,192]{5,0,3,2,1,4:T(2,128)} %all-to-all-done) | data formatting | bytes 10616832 | tf_op jit(solution)/shard_map/all_to_all | solution.py:289
  267.8 8.6 %copy.88 = f32[2,1,3,32,6,6,192]{6,0,5,4,3,2,1:T(2,128)} copy(f32[2,1,3,32,6,6,192]{6,0,5,3,4,2,1:T(2,128)} %bitcast.180) | data formatting | bytes 10616832 | tf_op jit(solution)/shard_map/all_to_all | solution.py:289
  276.4 9.5 %fusion.17 = f32[2,1,3,192,6,192]{5,3,4,2,0,1:T(8,128)S(1)} fusion(f32[2,3,192,6,192]{4,0,3,2,1:T(2,128)} %bitcast.178, f32[1,2,192,192]{2,3,0,1:T(8,128)S(1)} %get-tuple-element.36, f32[1,2,192,192]{2,3,0,1:T(8,128)} %get-tuple-element.37), kind=kOutput, calls=%fused_computation.31 | convolution fusion | flops 3057795072 | bytes 11206656 | tf_op jit(solution)/shard_map/pbckyz,pqkn->qbcnyz/dot_general | solution.py:80
  286.0 1.6 multiply_add_fusion.2
  287.6 1.2 copy-done
  288.7 3.5 pad_maximum_fusion
  292.3 8.7 %fusion.20 = f32[2,1,3,192,6,192]{5,3,4,2,0,1:T(8,128)} fusion(f32[2,3,192,6,192]{4,2,3,1,0:T(8,128)S(1)} %get-tuple-element.22, f32[1,2,192,192]{2,3,1,0:T(8,128)S(1)} %get-tuple-element.38, f32[1,2,192,192]{2,3,1,0:T(8,128)S(1)} %get-tuple-element.35), kind=kOutput, calls=%fused_computation.32 | convolution fusion | flops 3057795072 | bytes 11206656 | tf_op jit(solution)/shard_map/pbckyz,pqkn->qbcnyz/dot_general | solution.py:80
  301.0 11.4 %copy.92 = f32[2,1,3,192,6,192]{5,0,4,2,1,3:T(2,128)} copy(f32[2,1,3,192,6,192]{5,3,4,2,0,1:T(8,128)} %fusion.20) | data formatting | bytes 10616832 | tf_op jit(solution)/shard_map/pbckyz,pqkn->qbcnyz/transpose | solution.py:80
  312.4 3.6 all-to-all-start.1
  316.0 6.4 %multiply_reduce_fusion.2 = (f32[]{:T(128)}, f32[]{:T(128)}, f32[]{:T(128)}, f32[]{:T(128)}) fusion(f32[2,1,3,192,6,192]{5,3,4,2,0,1:T(8,128)} %copy-done, f32[2,1,3,192,6,192]{5,3,4,2,0,1:T(8,128)} %get-tuple-element.21), kind=kLoop, calls=%fused_computation.28 | loop fusion | flops 5308412 | bytes 10616848 | tf_op jit(solution)/shard_map/an,bn->ab/dot_general | solution.py:305
  324.9 167.7 %all-reduce = (f32[1,1]{1,0:T(1,128)}, f32[1,1]{1,0:T(1,128)}) all-reduce(f32[1,1]{1,0:T(1,128)} %bitcast.71, f32[1,1]{1,0:T(1,128)} %bitcast.68), channel_id=1, replica_groups=mesh['groups'=1,'wide'=32] {'wide'}, use_global_device_ids=true, to_apply=%region_3.4 | all-reduce | flops 2 | bytes 16 | tf_op jit(solution)/shard_map/psum | solution.py:311
  493.9 0.6 pad_maximum_fusion.6
  494.5 8.4 %copy.93 = f32[2,1,3,192,6,192]{5,0,4,3,2,1:T(2,128)} copy(f32[2,1,3,192,6,192]{5,0,4,2,1,3:T(2,128)} %all-to-all-done.1) | data formatting | bytes 10616832 | tf_op jit(solution)/shard_map/all_to_all | solution.py:292
  502.9 9.4 %copy.94 = f32[2,1,3,6,32,6,192]{6,0,5,4,3,2,1:T(2,128)} copy(f32[2,1,3,6,32,6,192]{6,0,5,3,4,2,1:T(2,128)} %bitcast.181) | data formatting | bytes 10616832 | tf_op jit(solution)/shard_map/all_to_all | solution.py:292
  512.2 9.2 %fusion.23 = f32[2,3,6,192,192]{4,3,2,1,0:T(8,128)S(1)} fusion(f32[2,3,6,192,192]{4,0,3,2,1:T(2,128)} %bitcast.179, f32[1,2,192,192]{2,3,1,0:T(8,128)S(1)} %get-tuple-element.38, f32[1,2,192,192]{2,3,1,0:T(8,128)S(1)} %get-tuple-element.35), kind=kOutput, calls=%fused_computation.33 | convolution fusion | flops 3057795072 | bytes 11206656 | tf_op jit(solution)/shard_map/pbcxkz,pqkn->qbcxnz/dot_general | solution.py:82
  521.5 6.1 %fusion.4 = f32[2,192,3,6,192,1]{4,1,5,3,2,0:T(8,128)S(1)} fusion(f32[2,3,6,192,192]{4,3,2,1,0:T(8,128)S(1)} %fusion.23, f32[1,2,192,192]{2,3,1,0:T(8,128)S(1)} %get-tuple-element.38, f32[1,2,192,192]{2,3,1,0:T(8,128)S(1)} %get-tuple-element.35), kind=kOutput, calls=%fused_computation.5 | convolution fusion | flops 3057795072 | bytes 11206656 | tf_op jit(solution)/shard_map/pbcxyk,pqkn->qbcxyn/dot_general | solution.py:83
  528.6 1.1 subtract_convert_fusion.1
  530.6 0.7 pad_maximum_fusion.1
  531.3 3.7 copy.101
  (40 shorter events, 3.6 us)
Async XLA Ops:
  37.4 1.3 collective-permute-start
  38.7 4.5 collective-permute-start.1
  43.1 3.7 collective-permute-start.2
  46.8 3.7 collective-permute-start.3
  50.5 4.7 collective-permute-start.4
  94.3 163.7 %all-to-all-start = ((f32[2,1,3,6,192,192]{5,0,3,2,1,4:T(2,128)}), f32[2,1,3,6,192,192]{5,0,3,2,1,4:T(2,128)}, u32[]{:S(2)}, u32[]{:S(2)}) async-start(f32[2,1,3,6,192,192]{5,0,3,2,1,4:T(2,128)} %copy.86), calls=%async_computation | async-start | bytes 14155776 | tf_op jit(solution)/shard_map/all_to_all | solution.py:289
  100.7 3.3 copy-start.1
  103.9 2.4 copy-start.6
  276.4 9.6 %copy-start.2 = (f32[192,6,192]{2,0,1:T(8,128)S(1)}, f32[192,6,192]{2,0,1:T(8,128)}, u32[]{:S(2)}) copy-start(f32[192,6,192]{2,0,1:T(8,128)} %get-tuple-element.34) | copy-start | bytes 2654212
  276.4 9.6 %copy-start.3 = (f32[192,6,192]{2,0,1:T(8,128)S(1)}, f32[192,6,192]{2,0,1:T(8,128)}, u32[]{:S(2)}) copy-start(f32[192,6,192]{2,0,1:T(8,128)} %get-tuple-element.23) | copy-start | bytes 2654212
  276.4 9.6 %copy-start.4 = (f32[192,6,192]{2,0,1:T(8,128)S(1)}, f32[192,6,192]{2,0,1:T(8,128)}, u32[]{:S(2)}) copy-start(f32[192,6,192]{2,0,1:T(8,128)} %get-tuple-element.24) | copy-start | bytes 2654212
  276.4 9.6 %copy-start.5 = (f32[192,6,192]{2,0,1:T(8,128)S(1)}, f32[192,6,192]{2,0,1:T(8,128)}, u32[]{:S(2)}) copy-start(f32[192,6,192]{2,0,1:T(8,128)} %get-tuple-element.25) | copy-start | bytes 2654212
  285.9 2.8 copy-start
  312.4 182.2 %all-to-all-start.1 = ((f32[2,1,3,192,6,192]{5,0,4,2,1,3:T(2,128)}), f32[2,1,3,192,6,192]{5,0,4,2,1,3:T(2,128)}, u32[]{:S(2)}, u32[]{:S(2)}) async-start(f32[2,1,3,192,6,192]{5,0,4,2,1,3:T(2,128)} %copy.92), calls=%async_computation.1 | async-start | bytes 14155776 | tf_op jit(solution)/shard_map/all_to_all | solution.py:292
  527.9 0.7 copy-start.7

commit v4 on v3

--- a/solution.py
+++ b/solution.py
@@ -109,7 +109,7 @@
     )
 
 
-def front_kernel(coef_ref, qx_ref, trial_ref, locked_ref, chi_ref, clo_ref, shi_ref, slo_ref, out_ref):
+def front_kernel(comps, coef_ref, qx_ref, trial_ref, locked_ref, chi_ref, clo_ref, shi_ref, slo_ref, out_ref):
     band = pl.program_id(0)
     plane = pl.program_id(1)
     kept = locked_ref.shape[0]
@@ -117,9 +117,10 @@
     f32 = jnp.float32
     first = [coef_ref[band, k] for k in range(kept)]
     second = [coef_ref[band, kept + k] for k in range(kept)]
-    part_re = []
-    part_im = []
-    for comp in range(3):
+    needed = sorted({(c + 1) % 3 for c in comps} | {(c + 2) % 3 for c in comps})
+    part_re = {}
+    part_im = {}
+    for comp in needed:
         acc_re = trial_ref[0, 0, comp, 0].astype(f32)
         acc_im = trial_ref[0, 1, comp, 0].astype(f32)
         for k in range(kept):
@@ -127,8 +128,8 @@
             l_im = locked_ref[k, 1, comp, 0].astype(f32)
             acc_re = acc_re - first[k] * l_re + second[k] * l_im
             acc_im = acc_im - first[k] * l_im - second[k] * l_re
-        part_re.append(acc_re)
-        part_im.append(acc_im)
+        part_re[comp] = acc_re
+        part_im[comp] = acc_im
     rows = lax.broadcasted_iota(jnp.int32, (size, 1), 0)
     cols = lax.broadcasted_iota(jnp.int32, (1, size), 1)
     half = size // 2
@@ -139,7 +140,7 @@
     c_lo = clo_ref[...]
     s_hi = shi_ref[...]
     s_lo = slo_ref[...]
-    for comp in range(3):
+    for slot, comp in enumerate(comps):
         a = (comp + 1) % 3
         b = (comp + 2) % 3
         cur_re = -(waves[a] * part_im[b] - waves[b] * part_im[a])
@@ -148,8 +149,8 @@
         z_im = dot_right(cur_re, s_hi, s_lo) + dot_right(cur_im, c_hi, c_lo)
         y_re = dot_left(c_hi, c_lo, z_re) - dot_left(s_hi, s_lo, z_im)
         y_im = dot_left(s_hi, s_lo, z_re) + dot_left(c_hi, c_lo, z_im)
-        out_ref[0, 0, comp, 0] = y_re
-        out_ref[1, 0, comp, 0] = y_im
+        out_ref[0, 0, slot, 0] = y_re
+        out_ref[1, 0, slot, 0] = y_im
 
 
 def numpy_split(table):
@@ -169,14 +170,15 @@
     return c_hi, c_lo, s_hi, s_lo
 
 
-def front_pass(coef_rows, wave_x, trial_bands, locked_bands):
+def front_pass(comps, coef_rows, wave_x, trial_bands, locked_bands):
     band_count, _, _, local_x, size, _ = trial_bands.shape
     kept = locked_bands.shape[0]
     tables = dft_tables(size, 1.0)
     smem = pl.BlockSpec(memory_space=pltpu.SMEM)
     table_spec = pl.BlockSpec((size, size), lambda b, x: (0, 0))
+    width = len(comps)
     return pl.pallas_call(
-        front_kernel,
+        functools.partial(front_kernel, comps),
         grid=(band_count, local_x),
         in_specs=[
             smem,
@@ -188,8 +190,8 @@
             table_spec,
             table_spec,
         ],
-        out_specs=pl.BlockSpec((2, 1, 3, 1, size, size), lambda b, x: (0, b, 0, x, 0, 0)),
-        out_shape=jax.ShapeDtypeStruct((2, band_count, 3, local_x, size, size), jnp.float32),
+        out_specs=pl.BlockSpec((2, 1, width, 1, size, size), lambda b, x: (0, b, 0, x, 0, 0)),
+        out_shape=jax.ShapeDtypeStruct((2, band_count, width, local_x, size, size), jnp.float32),
     )(coef_rows, wave_x, trial_bands, locked_bands, *tables)
 
 
@@ -248,14 +250,15 @@
     return lax.linalg.triangular_solve(lower, middle, left_side=True, lower=True, transpose_a=True)
 
 
-def maxwell_pass(curled, waves, inv_diag, inv_corr, to_space_fn, to_spectrum_fn):
-    moved = to_space_fn(curled)
-    space = transform(moved, 2, 1.0)
+def maxwell_pass(chunks, waves, inv_diag, inv_corr, to_space_fn, to_spectrum_fn):
+    space = jnp.concatenate([transform(to_space_fn(chunk), 2, 1.0) for chunk in chunks], axis=2)
     weighted = apply_tensor(space, inv_diag, inv_corr)
-    front = transform(weighted, 2, -1.0)
-    home = to_spectrum_fn(front)
-    home = transform(home, 3, -1.0)
-    home = transform(home, 4, -1.0)
+    homes = []
+    for comp in range(weighted.shape[2]):
+        home = to_spectrum_fn(transform(weighted[:, :, comp : comp + 1], 2, -1.0))
+        home = transform(home, 3, -1.0)
+        homes.append(transform(home, 4, -1.0))
+    home = jnp.concatenate(homes, axis=2)
     return (curl_times_i(waves, home), space, weighted)
 
 
@@ -291,8 +294,8 @@
     def send_home_one(field):
         return lax.all_to_all(field, "wide", split_axis=3, concat_axis=4, tiled=True)
 
-    curled = front_pass(coef.T, wave_x, trial_bands, locked_bands)
-    results = [maxwell_pass(curled, waves, inv_diag, inv_corr, send_out_one, send_home_one)]
+    chunks = [front_pass((comp,), coef.T, wave_x, trial_bands, locked_bands) for comp in range(3)]
+    results = [maxwell_pass(chunks, waves, inv_diag, inv_corr, send_out_one, send_home_one)]
     applied_st, space, weighted = [
         jnp.concatenate([entry[slot] for entry in results], axis=1) for slot in range(3)
     ]

time: 544 us -> 510 us (0.938)
  blocking collectives: 168 us -> 65.3 us
  waiting for transfers between devices: 156 us -> 210 us
  local copies, waits for them, and re-layouts: 88.8 us -> 70.9 us
  starting transfers between devices: 20.4 us -> 38 us
  Pallas kernels: 23.1 us -> 39 us
  other arithmetic: 24.3 us -> 18.5 us
    psum x1, blocking collectives: 168 us -> 65.3 us  [per_device(): total_re, total_im = lax.psum((part_re, part_im), 'wide')]
    all_to_all x1 -> x3, waiting for transfers between devices: 0.01 us -> 95 us  [send_home_one(): lax.all_to_all(field, 'wide', split_axis=3, concat_axis=4, tiled=True)]
    all_to_all x1 -> x3, waiting for transfers between devices: 149 us -> 108 us  [send_out_one(): lax.all_to_all(field, 'wide', split_axis=4, concat_axis=3, tiled=True)]
    pallas_call x1 -> x3, Pallas kernels: 23.1 us -> 39 us  [front_pass(): pl.pallas_call(functools.partial(front_kernel, comps), grid=(band_count,...]
    all_to_all x2 -> x3, local copies, waits for them, and re-layouts: 17.7 us -> 7.42 us  [send_home_one(): lax.all_to_all(field, 'wide', split_axis=3, concat_axis=4, tiled=True)]
    all_to_all x2 -> x6, local copies, waits for them, and re-layouts: 18.3 us -> 8.51 us  [send_out_one(): lax.all_to_all(field, 'wide', split_axis=4, concat_axis=3, tiled=True)]
    all_to_all x1 -> x3, starting transfers between devices: 6.31 us -> 15.1 us  [send_out_one(): lax.all_to_all(field, 'wide', split_axis=4, concat_axis=3, tiled=True)]
    all_to_all x1 -> x3, starting transfers between devices: 3.62 us -> 12.4 us  [send_home_one(): lax.all_to_all(field, 'wide', split_axis=3, concat_axis=4, tiled=True)]
  transfers between devices with their start and end apart: 7 -> 11, of which waited for: 6 -> 10; matrix products, arithmetic and copies ran while one was open for 3% -> 13% of each run, Pallas kernels for 0% -> 5%
where the time goes in v4:
time: 510 us; the launch traced here: 501 us
  waiting for transfers between devices  210 us (41%)
  local copies, waits for them, and re-layouts  70.9 us (14%)
  blocking collectives  65.3 us (13%)
  matrix products  53.8 us (11%)
  Pallas kernels  39 us (8%)
  starting transfers between devices  38 us (7%)
  other arithmetic  18.5 us (4%)
  between operations  5.45 us (1%)
    all_to_all x3, waiting for transfers between devices, send_out_one(): lax.all_to_all(field, 'wide', split_axis=4, concat_axis=3, tiled=True)  108 us
    all_to_all x3, waiting for transfers between devices, send_home_one(): lax.all_to_all(field, 'wide', split_axis=3, concat_axis=4, tiled=True)  95 us
    psum x1, blocking collectives, per_device(): total_re, total_im = lax.psum((part_re, part_im), 'wide')  65.3 us
    pallas_call x3, Pallas kernels, front_pass(): pl.pallas_call(functools.partial(front_kernel, comps), grid=(band_count,...  39 us
    dot_general x6, matrix products, transform(): jnp.einsum('pbckyz,pqkn->qbcnyz', stacked, table, precision=three_pass)  22 us
    dot_general x1, matrix products, per_device(): jnp.einsum('icxyz,jcxyz->ij', rows, rows, preferred_element_type=jnp.floa...  16.5 us
    all_to_all x3, starting transfers between devices, send_out_one(): lax.all_to_all(field, 'wide', split_axis=4, concat_axis=3, tiled=True)  15.1 us
    pallas_call x3, local copies, waits for them, and re-layouts, front_pass(): pl.pallas_call(functools.partial(front_kernel, comps), grid=(band_count,...  14.7 us
  transfers between devices with their start and end apart: 11, of which 10 were waited for; matrix products, arithmetic and copies ran while one was open for 13% of the time, Pallas kernels for 5%

profile of v4, /device:TPU:0, one launch (start us, length us, event | category | flops | bytes accessed | tf_op | source)
XLA Modules:
  0.0 500.8 jit_solution(13043642477896344554)
XLA Ops:
  0.6 5.7 %copy.342 = bf16[1,2,3,6,192,192]{5,1,4,3,2,0:T(2,128)(2,1)S(1)} copy(bf16[1,2,3,6,192,192]{5,4,3,2,1,0:T(8,128)(2,1)} %trial_ref.5) | data formatting | bytes 5308416 | tf_op args[0]
  6.3 13.6 %copy.240 = bf16[8,3,6,192,192]{4,0,3,2,1:T(8,128)(2,1)S(1)} copy(bf16[8,3,6,192,192]{4,3,2,1,0:T(8,128)(2,1)} %bitcast.335) | data formatting | bytes 21233664 | tf_op jit(solution)/shard_map/reshape | solution.py:271
  19.9 16.5 %fusion.75 = f32[10,10]{0,1:T(8,128)S(1)} fusion(bf16[2,3,6,192,192]{4,0,3,2,1:T(2,128)(2,1)S(1)} %bitcast.351, bf16[8,3,6,192,192]{4,0,3,2,1:T(8,128)(2,1)S(1)} %copy.240), kind=kOutput, calls=%fused_computation.95 | convolution fusion | flops 159252480 | bytes 13271440 | tf_op jit(solution)/shard_map/icxyz,jcxyz->ij/dot_general | solution.py:275
  37.8 2.8 collective-permute-start.1
  42.3 2.0 collective-permute-start.2
  46.0 2.1 collective-permute-start.3
  49.7 3.0 collective-permute-start.4
  58.9 12.9 %shard_map.168 = f32[2,1,1,6,192,192]{5,4,3,2,1,0:T(8,128)} custom-call(f32[1,8]{1,0:T(1,128)} %fusion.104.coef_ref, f32[6]{0:T(128)} %fusion.112.qx_ref, bf16[1,2,3,6,192,192]{5,4,3,2,1,0:T(8,128)(2,1)} %trial_ref.5, bf16[4,2,3,6,192,192]{5,4,3,2,1,0:T(8,128)(2,1)} %locked_ref.5, bf16[192,192]{1,0:T(8,128)(2,1)} %constant.126.clone.chi_ref, ...), custom_call_target="tpu_custom_call" | custom-call | tf_op jit(solution)/shard_map/pallas_call | solution.py:180
  71.9 4.9 copy.160
  76.8 6.4 %all-to-all-start.1 = ((f32[2,1,1,6,192,192]{5,0,3,2,1,4:T(2,128)}), f32[2,1,1,6,192,192]{5,0,3,2,1,4:T(2,128)S(1)}, u32[]{:S(2)}, u32[]{:S(2)}) async-start(f32[2,1,1,6,192,192]{5,0,3,2,1,4:T(2,128)} %copy.160), calls=%async_computation.1 | async-start | bytes 4718592 | tf_op jit(solution)/shard_map/all_to_all | solution.py:292
  83.2 13.1 %shard_map.167 = f32[2,1,1,6,192,192]{5,4,3,2,1,0:T(8,128)} custom-call(f32[1,8]{1,0:T(1,128)} %fusion.104.coef_ref, f32[6]{0:T(128)} %fusion.112.qx_ref, bf16[1,2,3,6,192,192]{5,4,3,2,1,0:T(8,128)(2,1)} %trial_ref.5, bf16[4,2,3,6,192,192]{5,4,3,2,1,0:T(8,128)(2,1)} %locked_ref.5, bf16[192,192]{1,0:T(8,128)(2,1)} %constant.126.clone.chi_ref, ...), custom_call_target="tpu_custom_call" | custom-call | tf_op jit(solution)/shard_map/pallas_call | solution.py:180
  96.2 4.9 copy.156
  101.2 36.5 %all-to-all-done.1 = f32[2,1,1,6,192,192]{5,0,3,2,1,4:T(2,128)S(1)} async-done(((f32[2,1,1,6,192,192]{5,0,3,2,1,4:T(2,128)}), f32[2,1,1,6,192,192]{5,0,3,2,1,4:T(2,128)S(1)}, u32[]{:S(2)}, u32[]{:S(2)}) %all-to-all-start.1) | async-done | bytes 1769504 | tf_op jit(solution)/shard_map/all_to_all | solution.py:292
  137.7 4.1 all-to-all-start
  141.8 13.1 %shard_map.169 = f32[2,1,1,6,192,192]{5,4,3,2,1,0:T(8,128)} custom-call(f32[1,8]{1,0:T(1,128)} %fusion.104.coef_ref, f32[6]{0:T(128)} %fusion.112.qx_ref, bf16[1,2,3,6,192,192]{5,4,3,2,1,0:T(8,128)(2,1)} %trial_ref.5, bf16[4,2,3,6,192,192]{5,4,3,2,1,0:T(8,128)(2,1)} %locked_ref.5, bf16[192,192]{1,0:T(8,128)(2,1)} %constant.126.clone.chi_ref, ...), custom_call_target="tpu_custom_call" | custom-call | tf_op jit(solution)/shard_map/pallas_call | solution.py:180
  154.9 4.9 copy.164
  159.8 36.5 %all-to-all-done = f32[2,1,1,6,192,192]{5,0,3,2,1,4:T(2,128)} async-done(((f32[2,1,1,6,192,192]{5,0,3,2,1,4:T(2,128)}), f32[2,1,1,6,192,192]{5,0,3,2,1,4:T(2,128)}, u32[]{:S(2)}, u32[]{:S(2)}) %all-to-all-start) | async-done | bytes 1769504 | tf_op jit(solution)/shard_map/all_to_all | solution.py:292
  196.4 4.6 all-to-all-start.2
  206.9 2.5 bitcast_multiply_fusion.11
  211.0 2.5 copy.157
  214.3 2.2 fusion.31
  216.5 3.6 fusion.33
  220.2 34.8 %all-to-all-done.2 = f32[2,1,1,6,192,192]{5,0,3,2,1,4:T(2,128)} async-done(((f32[2,1,1,6,192,192]{5,0,3,2,1,4:T(2,128)}), f32[2,1,1,6,192,192]{5,0,3,2,1,4:T(2,128)}, u32[]{:S(2)}, u32[]{:S(2)}) %all-to-all-start.2) | async-done | bytes 1769504 | tf_op jit(solution)/shard_map/all_to_all | solution.py:292
  255.0 2.8 copy.165
  260.0 6.4 %fusion.23 = (f32[2,192,6,192]{3,1,2,0:T(8,128)}, f32[2,192,6,192]{3,1,2,0:T(8,128)}, f32[2,192,6,192]{3,1,2,0:T(8,128)S(1)}, f32[2,192,6,192,1]{3,1,4,2,0:T(8,128)}) fusion(f32[2,192,6,192,1]{3,1,4,2,0:T(8,128)S(1)} %fusion.31, f32[2,192,6,192,1]{3,1,4,2,0:T(8,128)S(1)} %copy-done, f32[192,6,192]{2,0,1:T(8,128)} %get-tuple-element.25, ...), kind=kOutput, calls=%fused_computation.42 | convolution fusion | flops 1025998848 | bytes 18284544 | tf_op jit(solution)/shard_map/pbckyz,pqkn->qbcnyz/dot_general | solution.py:80
  266.4 2.3 fusion.66
  268.7 3.2 copy.186
  271.9 4.1 all-to-all-start.5
  276.0 3.7 fusion.57
  279.8 3.3 copy.178
  283.1 47.5 %all-to-all-done.5 = f32[2,1,1,192,6,192]{5,0,4,2,1,3:T(2,128)} async-done(((f32[2,1,1,192,6,192]{5,0,4,2,1,3:T(2,128)}), f32[2,1,1,192,6,192]{5,0,4,2,1,3:T(2,128)}, u32[]{:S(2)}, u32[]{:S(2)}) %all-to-all-start.5) | async-done | bytes 1769504 | tf_op jit(solution)/shard_map/all_to_all | solution.py:295
  330.5 4.1 all-to-all-start.4
  334.7 3.7 fusion.48
  338.4 3.3 copy.170
  341.7 47.5 %all-to-all-done.4 = f32[2,1,1,192,6,192]{5,0,4,2,1,3:T(2,128)} async-done(((f32[2,1,1,192,6,192]{5,0,4,2,1,3:T(2,128)}), f32[2,1,1,192,6,192]{5,0,4,2,1,3:T(2,128)}, u32[]{:S(2)}, u32[]{:S(2)}) %all-to-all-start.4) | async-done | bytes 1769504 | tf_op jit(solution)/shard_map/all_to_all | solution.py:295
  389.2 4.1 all-to-all-start.3
  393.4 3.0 pad_maximum_fusion.1
  403.2 65.3 %all-reduce = (f32[1,1]{1,0:T(1,128)}, f32[1,1]{1,0:T(1,128)}) all-reduce(f32[1,1]{1,0:T(1,128)} %bitcast.125, f32[1,1]{1,0:T(1,128)} %bitcast.122), channel_id=1, replica_groups=mesh['groups'=1,'wide'=32] {'wide'}, use_global_device_ids=true, to_apply=%region_3.4 | all-reduce | flops 2 | bytes 16 | tf_op jit(solution)/shard_map/psum | solution.py:314
  470.4 2.5 copy.187
  472.9 2.5 copy.179
  475.4 2.2 fusion.69
  477.6 2.1 fusion.72
  479.6 2.2 fusion.60
  481.9 3.5 fusion.63
  485.3 2.5 copy.171
  487.8 2.4 fusion.51
  490.3 2.1 fusion.54
  496.6 3.7 copy.194
  (83 shorter events, 31.9 us)
Async XLA Ops:
  36.5 1.3 collective-permute-start
  37.8 4.5 collective-permute-start.1
  42.3 3.7 collective-permute-start.2
  46.0 3.7 collective-permute-start.3
  49.7 4.7 collective-permute-start.4
  76.8 60.9 %all-to-all-start.1 = ((f32[2,1,1,6,192,192]{5,0,3,2,1,4:T(2,128)}), f32[2,1,1,6,192,192]{5,0,3,2,1,4:T(2,128)S(1)}, u32[]{:S(2)}, u32[]{:S(2)}) async-start(f32[2,1,1,6,192,192]{5,0,3,2,1,4:T(2,128)} %copy.160), calls=%async_computation.1 | async-start | bytes 4718592 | tf_op jit(solution)/shard_map/all_to_all | solution.py:292
  137.7 58.6 %all-to-all-start = ((f32[2,1,1,6,192,192]{5,0,3,2,1,4:T(2,128)}), f32[2,1,1,6,192,192]{5,0,3,2,1,4:T(2,128)}, u32[]{:S(2)}, u32[]{:S(2)}) async-start(f32[2,1,1,6,192,192]{5,0,3,2,1,4:T(2,128)} %copy.156), calls=%async_computation | async-start | bytes 4718592 | tf_op jit(solution)/shard_map/all_to_all | solution.py:292
  196.4 58.7 %all-to-all-start.2 = ((f32[2,1,1,6,192,192]{5,0,3,2,1,4:T(2,128)}), f32[2,1,1,6,192,192]{5,0,3,2,1,4:T(2,128)}, u32[]{:S(2)}, u32[]{:S(2)}) async-start(f32[2,1,1,6,192,192]{5,0,3,2,1,4:T(2,128)} %copy.164), calls=%async_computation.2 | async-start | bytes 4718592 | tf_op jit(solution)/shard_map/all_to_all | solution.py:292
  201.0 2.5 copy-start.5
  203.5 13.0 %copy-start.7 = (f32[1,2,192,192]{2,3,0,1:T(8,128)}, f32[1,2,192,192]{2,3,0,1:T(8,128)S(1)}, u32[]{:S(2)}) copy-start(f32[1,2,192,192]{2,3,0,1:T(8,128)S(1)} %get-tuple-element.37) | copy-start | bytes 884740
  203.5 3.4 copy-start.14
  255.0 3.7 copy-start.10
  255.0 3.7 copy-start.11
  255.0 3.7 copy-start.12
  255.0 3.7 copy-start.13
  257.8 1.7 copy-start
  257.8 1.8 copy-start.8
  257.8 2.1 copy-start.9
  266.4 2.3 copy-start.3
  271.9 58.6 %all-to-all-start.5 = ((f32[2,1,1,192,6,192]{5,0,4,2,1,3:T(2,128)}), f32[2,1,1,192,6,192]{5,0,4,2,1,3:T(2,128)}, u32[]{:S(2)}, u32[]{:S(2)}) async-start(f32[2,1,1,192,6,192]{5,0,4,2,1,3:T(2,128)} %copy.186), calls=%async_computation.5 | async-start | bytes 4718592 | tf_op jit(solution)/shard_map/all_to_all | solution.py:295
  330.5 58.7 %all-to-all-start.4 = ((f32[2,1,1,192,6,192]{5,0,4,2,1,3:T(2,128)}), f32[2,1,1,192,6,192]{5,0,4,2,1,3:T(2,128)}, u32[]{:S(2)}, u32[]{:S(2)}) async-start(f32[2,1,1,192,6,192]{5,0,4,2,1,3:T(2,128)} %copy.178), calls=%async_computation.4 | async-start | bytes 4718592 | tf_op jit(solution)/shard_map/all_to_all | solution.py:295
  389.2 96.1 %all-to-all-start.3 = ((f32[2,1,1,192,6,192]{5,0,4,2,1,3:T(2,128)}), f32[2,1,1,192,6,192]{5,0,4,2,1,3:T(2,128)}, u32[]{:S(2)}, u32[]{:S(2)}) async-start(f32[2,1,1,192,6,192]{5,0,4,2,1,3:T(2,128)} %copy.170), calls=%async_computation.3 | async-start | bytes 4718592 | tf_op jit(solution)/shard_map/all_to_all | solution.py:295
  393.3 3.1 copy-start.1
  393.4 3.8 copy-start.2
  393.4 4.5 copy-start.4
  490.3 2.1 copy-start.6
  493.0 0.8 copy-start.15

commit v5 on v4

--- a/solution.py
+++ b/solution.py
@@ -311,7 +311,7 @@
     part_im = jnp.einsum("an,bn->ab", left_re, right_im, precision=highest) - jnp.einsum(
         "an,bn->ab", left_im, right_re, precision=highest
     )
-    total_re, total_im = lax.psum((part_re, part_im), "wide")
+    total_re, total_im = butterfly_sum(jnp.stack([part_re, part_im], axis=0), "wide", wide_count)
     rayleigh = jnp.stack([total_re * scale_all, total_im * scale_all], axis=0)
     return (applied, rayleigh)
 

time: 510 us -> 490 us (0.961)
  blocking collectives: 65.3 us -> 0 us
  waiting for transfers between devices: 210 us -> 244 us
  starting transfers between devices: 38 us -> 47.6 us
    psum x1 -> x0, blocking collectives: 65.3 us -> none  [per_device(): total_re, total_im = lax.psum((part_re, part_im), 'wide')]
    ppermute x5 -> x10, waiting for transfers between devices: 6.81 us -> 41.4 us  [butterfly_sum(): values = values + lax.ppermute(values, axis, pairs)]
    ppermute x5 -> x10, starting transfers between devices: 10.5 us -> 20.1 us  [butterfly_sum(): values = values + lax.ppermute(values, axis, pairs)]
  transfers between devices with their start and end apart: 11 -> 16, of which waited for: 10 -> 15; matrix products, arithmetic and copies ran while one was open for 13% -> 13% of each run, Pallas kernels for 5% -> 5%
where the time goes in v5:
time: 490 us; the launch traced here: 481 us
  waiting for transfers between devices  244 us (50%)
  local copies, waits for them, and re-layouts  71.5 us (15%)
  matrix products  53.7 us (11%)
  starting transfers between devices  47.6 us (10%)
  Pallas kernels  39 us (8%)
  other arithmetic  19 us (4%)
  between operations  5.39 us (1%)
    all_to_all x3, waiting for transfers between devices, send_out_one(): lax.all_to_all(field, 'wide', split_axis=4, concat_axis=3, tiled=True)  108 us
    all_to_all x3, waiting for transfers between devices, send_home_one(): lax.all_to_all(field, 'wide', split_axis=3, concat_axis=4, tiled=True)  95.1 us
    ppermute x10, waiting for transfers between devices, butterfly_sum(): values = values + lax.ppermute(values, axis, pairs)  41.4 us
    pallas_call x3, Pallas kernels, front_pass(): pl.pallas_call(functools.partial(front_kernel, comps), grid=(band_count,...  39 us
    dot_general x6, matrix products, transform(): jnp.einsum('pbckyz,pqkn->qbcnyz', stacked, table, precision=three_pass)  21.9 us
    ppermute x10, starting transfers between devices, butterfly_sum(): values = values + lax.ppermute(values, axis, pairs)  20.1 us
    dot_general x1, matrix products, per_device(): jnp.einsum('icxyz,jcxyz->ij', rows, rows, preferred_element_type=jnp.floa...  16.5 us
    all_to_all x3, starting transfers between devices, send_out_one(): lax.all_to_all(field, 'wide', split_axis=4, concat_axis=3, tiled=True)  15.1 us
  transfers between devices with their start and end apart: 16, of which 15 were waited for; matrix products, arithmetic and copies ran while one was open for 13% of the time, Pallas kernels for 5%

profile of v5, /device:TPU:0, one launch (start us, length us, event | category | flops | bytes accessed | tf_op | source)
XLA Modules:
  0.0 480.7 jit_solution(2639601651516060346)
XLA Ops:
  0.6 5.7 %copy.338 = bf16[1,2,3,6,192,192]{5,1,4,3,2,0:T(2,128)(2,1)S(1)} copy(bf16[1,2,3,6,192,192]{5,4,3,2,1,0:T(8,128)(2,1)} %trial_ref.5) | data formatting | bytes 5308416 | tf_op args[0]
  6.3 13.6 %copy.236 = bf16[8,3,6,192,192]{4,0,3,2,1:T(8,128)(2,1)S(1)} copy(bf16[8,3,6,192,192]{4,3,2,1,0:T(8,128)(2,1)} %bitcast.331) | data formatting | bytes 21233664 | tf_op jit(solution)/shard_map/reshape | solution.py:271
  19.9 16.5 %fusion.75 = f32[10,10]{0,1:T(8,128)S(1)} fusion(bf16[2,3,6,192,192]{4,0,3,2,1:T(2,128)(2,1)S(1)} %bitcast.347, bf16[8,3,6,192,192]{4,0,3,2,1:T(8,128)(2,1)S(1)} %copy.236), kind=kOutput, calls=%fused_computation.95 | convolution fusion | flops 159252480 | bytes 13271440 | tf_op jit(solution)/shard_map/icxyz,jcxyz->ij/dot_general | solution.py:275
  37.8 2.8 collective-permute-start.1
  49.7 3.0 collective-permute-start.4
  58.9 12.9 %shard_map.168 = f32[2,1,1,6,192,192]{5,4,3,2,1,0:T(8,128)} custom-call(f32[1,8]{1,0:T(1,128)} %fusion.104.coef_ref, f32[6]{0:T(128)} %fusion.112.qx_ref, bf16[1,2,3,6,192,192]{5,4,3,2,1,0:T(8,128)(2,1)} %trial_ref.5, bf16[4,2,3,6,192,192]{5,4,3,2,1,0:T(8,128)(2,1)} %locked_ref.5, bf16[192,192]{1,0:T(8,128)(2,1)} %constant.128.clone.chi_ref, ...), custom_call_target="tpu_custom_call" | custom-call | tf_op jit(solution)/shard_map/pallas_call | solution.py:180
  71.9 4.9 %copy.157 = f32[2,1,1,6,192,192]{5,0,3,2,1,4:T(2,128)} copy(f32[2,1,1,6,192,192]{5,4,3,2,1,0:T(8,128)} %shard_map.168) | data formatting | bytes 3538944 | tf_op jit(solution)/shard_map/pallas_call | solution.py:180
  76.8 6.4 %all-to-all-start.1 = ((f32[2,1,1,6,192,192]{5,0,3,2,1,4:T(2,128)}), f32[2,1,1,6,192,192]{5,0,3,2,1,4:T(2,128)S(1)}, u32[]{:S(2)}, u32[]{:S(2)}) async-start(f32[2,1,1,6,192,192]{5,0,3,2,1,4:T(2,128)} %copy.157), calls=%async_computation.1 | async-start | bytes 4718592 | tf_op jit(solution)/shard_map/all_to_all | solution.py:292
  83.2 13.0 %shard_map.167 = f32[2,1,1,6,192,192]{5,4,3,2,1,0:T(8,128)} custom-call(f32[1,8]{1,0:T(1,128)} %fusion.104.coef_ref, f32[6]{0:T(128)} %fusion.112.qx_ref, bf16[1,2,3,6,192,192]{5,4,3,2,1,0:T(8,128)(2,1)} %trial_ref.5, bf16[4,2,3,6,192,192]{5,4,3,2,1,0:T(8,128)(2,1)} %locked_ref.5, bf16[192,192]{1,0:T(8,128)(2,1)} %constant.128.clone.chi_ref, ...), custom_call_target="tpu_custom_call" | custom-call | tf_op jit(solution)/shard_map/pallas_call | solution.py:180
  96.2 4.9 %copy.153 = f32[2,1,1,6,192,192]{5,0,3,2,1,4:T(2,128)} copy(f32[2,1,1,6,192,192]{5,4,3,2,1,0:T(8,128)} %shard_map.167) | data formatting | bytes 3538944 | tf_op jit(solution)/shard_map/pallas_call | solution.py:180
  101.2 36.6 %all-to-all-done.1 = f32[2,1,1,6,192,192]{5,0,3,2,1,4:T(2,128)S(1)} async-done(((f32[2,1,1,6,192,192]{5,0,3,2,1,4:T(2,128)}), f32[2,1,1,6,192,192]{5,0,3,2,1,4:T(2,128)S(1)}, u32[]{:S(2)}, u32[]{:S(2)}) %all-to-all-start.1) | async-done | bytes 1769504 | tf_op jit(solution)/shard_map/all_to_all | solution.py:292
  137.7 4.1 all-to-all-start
  141.9 13.1 %shard_map.169 = f32[2,1,1,6,192,192]{5,4,3,2,1,0:T(8,128)} custom-call(f32[1,8]{1,0:T(1,128)} %fusion.104.coef_ref, f32[6]{0:T(128)} %fusion.112.qx_ref, bf16[1,2,3,6,192,192]{5,4,3,2,1,0:T(8,128)(2,1)} %trial_ref.5, bf16[4,2,3,6,192,192]{5,4,3,2,1,0:T(8,128)(2,1)} %locked_ref.5, bf16[192,192]{1,0:T(8,128)(2,1)} %constant.128.clone.chi_ref, ...), custom_call_target="tpu_custom_call" | custom-call | tf_op jit(solution)/shard_map/pallas_call | solution.py:180
  154.9 4.9 %copy.161 = f32[2,1,1,6,192,192]{5,0,3,2,1,4:T(2,128)} copy(f32[2,1,1,6,192,192]{5,4,3,2,1,0:T(8,128)} %shard_map.169) | data formatting | bytes 3538944 | tf_op jit(solution)/shard_map/pallas_call | solution.py:180
  159.8 36.5 %all-to-all-done = f32[2,1,1,6,192,192]{5,0,3,2,1,4:T(2,128)} async-done(((f32[2,1,1,6,192,192]{5,0,3,2,1,4:T(2,128)}), f32[2,1,1,6,192,192]{5,0,3,2,1,4:T(2,128)}, u32[]{:S(2)}, u32[]{:S(2)}) %all-to-all-start) | async-done | bytes 1769504 | tf_op jit(solution)/shard_map/all_to_all | solution.py:292
  196.4 4.6 all-to-all-start.2
  206.9 2.5 bitcast_multiply_fusion.11
  211.1 2.5 copy.154
  214.4 2.2 fusion.31
  216.6 3.6 fusion.33
  220.2 34.8 %all-to-all-done.2 = f32[2,1,1,6,192,192]{5,0,3,2,1,4:T(2,128)} async-done(((f32[2,1,1,6,192,192]{5,0,3,2,1,4:T(2,128)}), f32[2,1,1,6,192,192]{5,0,3,2,1,4:T(2,128)}, u32[]{:S(2)}, u32[]{:S(2)}) %all-to-all-start.2) | async-done | bytes 1769504 | tf_op jit(solution)/shard_map/all_to_all | solution.py:292
  255.0 2.8 copy.162
  260.0 6.4 %fusion.23 = (f32[2,192,6,192]{3,1,2,0:T(8,128)}, f32[2,192,6,192]{3,1,2,0:T(8,128)}, f32[2,192,6,192]{3,1,2,0:T(8,128)S(1)}, f32[2,192,6,192,1]{3,1,4,2,0:T(8,128)}) fusion(f32[2,192,6,192,1]{3,1,4,2,0:T(8,128)S(1)} %fusion.31, f32[2,192,6,192,1]{3,1,4,2,0:T(8,128)S(1)} %copy-done, f32[192,6,192]{2,0,1:T(8,128)} %get-tuple-element.23, ...), kind=kOutput, calls=%fused_computation.42 | convolution fusion | flops 1025998848 | bytes 18284544 | tf_op jit(solution)/shard_map/pbckyz,pqkn->qbcnyz/dot_general | solution.py:80
  266.4 2.3 fusion.66
  268.6 3.3 copy.183
  271.9 4.1 all-to-all-start.5
  276.0 3.7 fusion.57
  279.8 3.2 copy.175
  283.0 47.6 %all-to-all-done.5 = f32[2,1,1,192,6,192]{5,0,4,2,1,3:T(2,128)} async-done(((f32[2,1,1,192,6,192]{5,0,4,2,1,3:T(2,128)}), f32[2,1,1,192,6,192]{5,0,4,2,1,3:T(2,128)}, u32[]{:S(2)}, u32[]{:S(2)}) %all-to-all-start.5) | async-done | bytes 1769504 | tf_op jit(solution)/shard_map/all_to_all | solution.py:295
  330.5 4.1 all-to-all-start.4
  334.7 3.7 fusion.48
  338.4 3.3 copy.167
  341.7 47.5 %all-to-all-done.4 = f32[2,1,1,192,6,192]{5,0,4,2,1,3:T(2,128)} async-done(((f32[2,1,1,192,6,192]{5,0,4,2,1,3:T(2,128)}), f32[2,1,1,192,6,192]{5,0,4,2,1,3:T(2,128)}, u32[]{:S(2)}, u32[]{:S(2)}) %all-to-all-start.4) | async-done | bytes 1769504 | tf_op jit(solution)/shard_map/all_to_all | solution.py:295
  389.2 4.1 all-to-all-start.3
  393.4 3.0 pad_maximum_fusion.1
  398.6 2.2 multiply_reduce_fusion.2
  408.3 2.3 collective-permute-start.7
  413.5 19.1 %collective-permute-done.8 = f32[2,1,1]{0,2,1:T(1,128)S(1)} collective-permute-done((f32[2,1,1]{0,2,1:T(1,128)S(1)}, f32[2,1,1]{0,2,1:T(1,128)S(1)}, u32[]{:S(2)}, u32[]{:S(2)}) %collective-permute-start.8) | collective-permute-done | bytes 40 | tf_op jit(solution)/shard_map/ppermute | solution.py:204
  432.6 4.0 collective-permute-start.9
  436.6 11.2 %collective-permute-done.9 = f32[2,1,1]{0,2,1:T(1,128)S(1)} collective-permute-done((f32[2,1,1]{0,2,1:T(1,128)S(1)}, f32[2,1,1]{0,2,1:T(1,128)S(1)}, u32[]{:S(2)}, u32[]{:S(2)}) %collective-permute-start.9) | collective-permute-done | bytes 40 | tf_op jit(solution)/shard_map/ppermute | solution.py:204
  450.3 2.5 copy.184
  452.8 2.5 copy.176
  455.3 2.2 fusion.69
  459.6 2.2 fusion.60
  461.8 3.5 fusion.63
  465.3 2.5 copy.168
  467.7 2.4 fusion.51
  476.5 3.7 copy.190
  (99 shorter events, 46.6 us)
Async XLA Ops:
  36.5 1.3 collective-permute-start
  37.8 4.5 collective-permute-start.1
  42.3 3.7 collective-permute-start.2
  46.0 3.7 collective-permute-start.3
  49.7 4.7 collective-permute-start.4
  76.8 60.9 %all-to-all-start.1 = ((f32[2,1,1,6,192,192]{5,0,3,2,1,4:T(2,128)}), f32[2,1,1,6,192,192]{5,0,3,2,1,4:T(2,128)S(1)}, u32[]{:S(2)}, u32[]{:S(2)}) async-start(f32[2,1,1,6,192,192]{5,0,3,2,1,4:T(2,128)} %copy.157), calls=%async_computation.1 | async-start | bytes 4718592 | tf_op jit(solution)/shard_map/all_to_all | solution.py:292
  137.7 58.6 %all-to-all-start = ((f32[2,1,1,6,192,192]{5,0,3,2,1,4:T(2,128)}), f32[2,1,1,6,192,192]{5,0,3,2,1,4:T(2,128)}, u32[]{:S(2)}, u32[]{:S(2)}) async-start(f32[2,1,1,6,192,192]{5,0,3,2,1,4:T(2,128)} %copy.153), calls=%async_computation | async-start | bytes 4718592 | tf_op jit(solution)/shard_map/all_to_all | solution.py:292
  196.4 58.7 %all-to-all-start.2 = ((f32[2,1,1,6,192,192]{5,0,3,2,1,4:T(2,128)}), f32[2,1,1,6,192,192]{5,0,3,2,1,4:T(2,128)}, u32[]{:S(2)}, u32[]{:S(2)}) async-start(f32[2,1,1,6,192,192]{5,0,3,2,1,4:T(2,128)} %copy.161), calls=%async_computation.2 | async-start | bytes 4718592 | tf_op jit(solution)/shard_map/all_to_all | solution.py:292
  201.0 2.5 copy-start.5
  203.5 13.1 %copy-start.7 = (f32[1,2,192,192]{2,3,0,1:T(8,128)}, f32[1,2,192,192]{2,3,0,1:T(8,128)S(1)}, u32[]{:S(2)}) copy-start(f32[1,2,192,192]{2,3,0,1:T(8,128)S(1)} %get-tuple-element.35) | copy-start | bytes 884740
  203.5 3.4 copy-start.14
  255.0 3.7 copy-start.10
  255.0 3.7 copy-start.11
  255.0 3.7 copy-start.12
  255.0 3.7 copy-start.13
  257.8 1.7 copy-start
  257.8 1.8 copy-start.8
  257.9 2.1 copy-start.9
  266.3 2.3 copy-start.3
  271.9 58.7 %all-to-all-start.5 = ((f32[2,1,1,192,6,192]{5,0,4,2,1,3:T(2,128)}), f32[2,1,1,192,6,192]{5,0,4,2,1,3:T(2,128)}, u32[]{:S(2)}, u32[]{:S(2)}) async-start(f32[2,1,1,192,6,192]{5,0,4,2,1,3:T(2,128)} %copy.183), calls=%async_computation.5 | async-start | bytes 4718592 | tf_op jit(solution)/shard_map/all_to_all | solution.py:295
  330.5 58.7 %all-to-all-start.4 = ((f32[2,1,1,192,6,192]{5,0,4,2,1,3:T(2,128)}), f32[2,1,1,192,6,192]{5,0,4,2,1,3:T(2,128)}, u32[]{:S(2)}, u32[]{:S(2)}) async-start(f32[2,1,1,192,6,192]{5,0,4,2,1,3:T(2,128)} %copy.175), calls=%async_computation.4 | async-start | bytes 4718592 | tf_op jit(solution)/shard_map/all_to_all | solution.py:295
  389.2 76.1 %all-to-all-start.3 = ((f32[2,1,1,192,6,192]{5,0,4,2,1,3:T(2,128)}), f32[2,1,1,192,6,192]{5,0,4,2,1,3:T(2,128)}, u32[]{:S(2)}, u32[]{:S(2)}) async-start(f32[2,1,1,192,6,192]{5,0,4,2,1,3:T(2,128)} %copy.167), calls=%async_computation.3 | async-start | bytes 4718592 | tf_op jit(solution)/shard_map/all_to_all | solution.py:295
  393.3 3.1 copy-start.1
  393.3 3.8 copy-start.2
  393.4 4.5 copy-start.4
  403.4 1.1 collective-permute-start.5
  404.6 3.6 collective-permute-start.6
  408.3 3.8 collective-permute-start.7
  412.1 20.5 %collective-permute-start.8 = (f32[2,1,1]{0,2,1:T(1,128)S(1)}, f32[2,1,1]{0,2,1:T(1,128)S(1)}, u32[]{:S(2)}, u32[]{:S(2)}) collective-permute-start(f32[2,1,1]{0,2,1:T(1,128)S(1)} %add.202), channel_id=1, source_target_pairs={{0,8},{1,9},{2,10},{3,11},{4,12},{5,13},{6,14},{7,15},{8,0},{9,1},... | collective-permute-start | bytes 32 | tf_op jit(solution)/shard_map/ppermute | solution.py:204
  432.6 15.3 %collective-permute-start.9 = (f32[2,1,1]{0,2,1:T(1,128)S(1)}, f32[2,1,1]{0,2,1:T(1,128)S(1)}, u32[]{:S(2)}, u32[]{:S(2)}) collective-permute-start(f32[2,1,1]{0,2,1:T(1,128)S(1)} %add.203), channel_id=1, source_target_pairs={{0,16},{1,17},{2,18},{3,19},{4,20},{5,21},{6,22},{7,23},{8,24},{9,... | collective-permute-start | bytes 32 | tf_op jit(solution)/shard_map/ppermute | solution.py:204
  470.2 2.1 copy-start.6
  472.9 0.8 copy-start.15

commit v6 on v5

--- a/solution.py
+++ b/solution.py
@@ -253,12 +253,9 @@
 def maxwell_pass(chunks, waves, inv_diag, inv_corr, to_space_fn, to_spectrum_fn):
     space = jnp.concatenate([transform(to_space_fn(chunk), 2, 1.0) for chunk in chunks], axis=2)
     weighted = apply_tensor(space, inv_diag, inv_corr)
-    homes = []
-    for comp in range(weighted.shape[2]):
-        home = to_spectrum_fn(transform(weighted[:, :, comp : comp + 1], 2, -1.0))
-        home = transform(home, 3, -1.0)
-        homes.append(transform(home, 4, -1.0))
-    home = jnp.concatenate(homes, axis=2)
+    home = to_spectrum_fn(transform(weighted, 2, -1.0))
+    home = transform(home, 3, -1.0)
+    home = transform(home, 4, -1.0)
     return (curl_times_i(waves, home), space, weighted)
 
 

time: 490 us -> 507 us (1.035)
  local copies, waits for them, and re-layouts: 71.5 us -> 87 us
  waiting for transfers between devices: 244 us -> 257 us
  starting transfers between devices: 47.6 us -> 36 us
    ppermute x10, waiting for transfers between devices: 41.4 us -> 149 us  [butterfly_sum(): values = values + lax.ppermute(values, axis, pairs)]
    all_to_all x3 -> x1, waiting for transfers between devices: 95.1 us -> 0.01 us  [send_home_one(): lax.all_to_all(field, 'wide', split_axis=3, concat_axis=4, tiled=True)]
    all_to_all x3 -> x2, local copies, waits for them, and re-layouts: 7.42 us -> 17.7 us  [send_home_one(): lax.all_to_all(field, 'wide', split_axis=3, concat_axis=4, tiled=True)]
    all_to_all x3 -> x1, starting transfers between devices: 12.4 us -> 4.35 us  [send_home_one(): lax.all_to_all(field, 'wide', split_axis=3, concat_axis=4, tiled=True)]
    reshape x1, local copies, waits for them, and re-layouts: 13.6 us -> 20.2 us  [per_device(): locked_bands.reshape((2 * kept_count,) + locked_bands.shape[2:])]
    dot_general x6 -> x4, matrix products: 21.9 us -> 16.4 us  [transform(): jnp.einsum('pbckyz,pqkn->qbcnyz', stacked, table, precision=three_pass)]
    unnamed x34 -> x44, local copies, waits for them, and re-layouts: 13.7 us -> 11.1 us
    transpose x3 -> x1, local copies, waits for them, and re-layouts: 9.73 us -> 11.4 us  [transform(): jnp.einsum('pbckyz,pqkn->qbcnyz', stacked, table, precision=three_pass)]
  transfers between devices with their start and end apart: 16 -> 14, of which waited for: 15 -> 13; matrix products, arithmetic and copies ran while one was open for 13% -> 7% of each run, Pallas kernels for 5% -> 5%
where the time goes in v6:
time: 507 us; the launch traced here: 497 us
  waiting for transfers between devices  257 us (51%)
  local copies, waits for them, and re-layouts  87 us (17%)
  matrix products  50 us (10%)
  Pallas kernels  39 us (8%)
  starting transfers between devices  36 us (7%)
  other arithmetic  22.8 us (4%)
  between operations  5.36 us (1%)
    ppermute x10, waiting for transfers between devices, butterfly_sum(): values = values + lax.ppermute(values, axis, pairs)  149 us
    all_to_all x3, waiting for transfers between devices, send_out_one(): lax.all_to_all(field, 'wide', split_axis=4, concat_axis=3, tiled=True)  108 us
    pallas_call x3, Pallas kernels, front_pass(): pl.pallas_call(functools.partial(front_kernel, comps), grid=(band_count,...  39 us
    reshape x1, local copies, waits for them, and re-layouts, per_device(): locked_bands.reshape((2 * kept_count,) + locked_bands.shape[2:])  20.2 us
    all_to_all x2, local copies, waits for them, and re-layouts, send_home_one(): lax.all_to_all(field, 'wide', split_axis=3, concat_axis=4, tiled=True)  17.7 us
    dot_general x1, matrix products, per_device(): jnp.einsum('icxyz,jcxyz->ij', rows, rows, preferred_element_type=jnp.floa...  17.3 us
    ppermute x10, starting transfers between devices, butterfly_sum(): values = values + lax.ppermute(values, axis, pairs)  16.6 us
    dot_general x4, matrix products, transform(): jnp.einsum('pbckyz,pqkn->qbcnyz', stacked, table, precision=three_pass)  16.4 us
  transfers between devices with their start and end apart: 14, of which 13 were waited for; matrix products, arithmetic and copies ran while one was open for 7% of the time, Pallas kernels for 5%

profile of v6, /device:TPU:0, one launch (start us, length us, event | category | flops | bytes accessed | tf_op | source)
XLA Modules:
  0.0 497.0 jit_solution(1978187756930028084)
XLA Ops:
  0.6 20.2 %copy.163 = bf16[8,3,6,192,192]{4,0,3,2,1:T(8,128)(2,1)} copy(bf16[8,3,6,192,192]{4,3,2,1,0:T(8,128)(2,1)} %bitcast.236) | data formatting | bytes 21233664 | tf_op jit(solution)/shard_map/reshape | solution.py:268
  20.8 3.7 copy.200
  24.5 17.3 %fusion.39 = f32[10,10]{0,1:T(8,128)S(1)} fusion(bf16[2,3,6,192,192]{4,0,3,2,1:T(2,128)(2,1)S(1)} %bitcast.252, bf16[8,3,6,192,192]{4,0,3,2,1:T(8,128)(2,1)} %copy.163), kind=kOutput, calls=%fused_computation.72 | convolution fusion | flops 159252480 | bytes 13271440 | tf_op jit(solution)/shard_map/icxyz,jcxyz->ij/dot_general | solution.py:272
  43.1 2.8 collective-permute-start.1
  46.0 1.6 collective-permute-done.1
  47.6 2.1 collective-permute-start.2
  49.6 1.6 collective-permute-done.2
  51.3 2.1 collective-permute-start.3
  53.4 1.6 collective-permute-done.3
  55.0 3.0 collective-permute-start.4
  64.3 13.0 %shard_map.167 = f32[2,1,1,6,192,192]{5,4,3,2,1,0:T(8,128)} custom-call(f32[1,8]{1,0:T(1,128)} %fusion.62.coef_ref, f32[6]{0:T(128)} %fusion.70.qx_ref, bf16[1,2,3,6,192,192]{5,4,3,2,1,0:T(8,128)(2,1)} %trial_ref.5, bf16[4,2,3,6,192,192]{5,4,3,2,1,0:T(8,128)(2,1)} %locked_ref.5, bf16[192,192]{1,0:T(8,128)(2,1)} %constant.110.clone.chi_ref, ...), custom_call_target="tpu_custom_call" | custom-call | tf_op jit(solution)/shard_map/pallas_call | solution.py:180
  77.3 4.9 copy.107
  82.2 6.4 %all-to-all-start = ((f32[2,1,1,6,192,192]{5,0,3,2,1,4:T(2,128)}), f32[2,1,1,6,192,192]{5,0,3,2,1,4:T(2,128)S(1)}, u32[]{:S(2)}, u32[]{:S(2)}) async-start(f32[2,1,1,6,192,192]{5,0,3,2,1,4:T(2,128)} %copy.107), calls=%async_computation | async-start | bytes 4718592 | tf_op jit(solution)/shard_map/all_to_all | solution.py:289
  88.6 13.0 %shard_map.168 = f32[2,1,1,6,192,192]{5,4,3,2,1,0:T(8,128)} custom-call(f32[1,8]{1,0:T(1,128)} %fusion.62.coef_ref, f32[6]{0:T(128)} %fusion.70.qx_ref, bf16[1,2,3,6,192,192]{5,4,3,2,1,0:T(8,128)(2,1)} %trial_ref.5, bf16[4,2,3,6,192,192]{5,4,3,2,1,0:T(8,128)(2,1)} %locked_ref.5, bf16[192,192]{1,0:T(8,128)(2,1)} %constant.110.clone.chi_ref, ...), custom_call_target="tpu_custom_call" | custom-call | tf_op jit(solution)/shard_map/pallas_call | solution.py:180
  101.6 4.9 copy.111
  106.5 36.7 %all-to-all-done = f32[2,1,1,6,192,192]{5,0,3,2,1,4:T(2,128)S(1)} async-done(((f32[2,1,1,6,192,192]{5,0,3,2,1,4:T(2,128)}), f32[2,1,1,6,192,192]{5,0,3,2,1,4:T(2,128)S(1)}, u32[]{:S(2)}, u32[]{:S(2)}) %all-to-all-start) | async-done | bytes 1769504 | tf_op jit(solution)/shard_map/all_to_all | solution.py:289
  143.2 4.1 all-to-all-start.1
  147.3 13.1 %shard_map.169 = f32[2,1,1,6,192,192]{5,4,3,2,1,0:T(8,128)} custom-call(f32[1,8]{1,0:T(1,128)} %fusion.62.coef_ref, f32[6]{0:T(128)} %fusion.70.qx_ref, bf16[1,2,3,6,192,192]{5,4,3,2,1,0:T(8,128)(2,1)} %trial_ref.5, bf16[4,2,3,6,192,192]{5,4,3,2,1,0:T(8,128)(2,1)} %locked_ref.5, bf16[192,192]{1,0:T(8,128)(2,1)} %constant.110.clone.chi_ref, ...), custom_call_target="tpu_custom_call" | custom-call | tf_op jit(solution)/shard_map/pallas_call | solution.py:180
  160.3 4.9 copy.115
  165.3 36.5 %all-to-all-done.1 = f32[2,1,1,6,192,192]{5,0,3,2,1,4:T(2,128)} async-done(((f32[2,1,1,6,192,192]{5,0,3,2,1,4:T(2,128)}), f32[2,1,1,6,192,192]{5,0,3,2,1,4:T(2,128)}, u32[]{:S(2)}, u32[]{:S(2)}) %all-to-all-start.1) | async-done | bytes 1769504 | tf_op jit(solution)/shard_map/all_to_all | solution.py:289
  201.8 4.5 all-to-all-start.2
  208.9 1.9 slice_bitcast_fusion.8
  210.8 1.8 copy-done.17
  212.6 2.4 bitcast_multiply_fusion.11
  216.6 2.5 copy.112
  219.9 2.2 fusion.33
  222.2 3.6 fusion.31
  225.8 34.6 %all-to-all-done.2 = f32[2,1,1,6,192,192]{5,0,3,2,1,4:T(2,128)} async-done(((f32[2,1,1,6,192,192]{5,0,3,2,1,4:T(2,128)}), f32[2,1,1,6,192,192]{5,0,3,2,1,4:T(2,128)}, u32[]{:S(2)}, u32[]{:S(2)}) %all-to-all-start.2) | async-done | bytes 1769504 | tf_op jit(solution)/shard_map/all_to_all | solution.py:289
  260.4 2.6 copy.116
  264.2 2.2 fusion.26
  267.2 1.4 fusion.21
  268.7 3.5 pad_maximum_fusion
  272.2 8.3 %fusion.14 = f32[2,1,3,192,6,192]{5,3,4,2,0,1:T(8,128)} fusion(f32[2,3,192,6,192]{4,2,3,0,1:T(8,128)S(1)} %get-tuple-element.20, f32[1,2,192,192]{2,3,1,0:T(8,128)S(1)} %get-tuple-element.36, f32[1,2,192,192]{2,3,1,0:T(8,128)S(1)} %get-tuple-element.33), kind=kOutput, calls=%fused_computation.29 | convolution fusion | flops 3057795072 | bytes 11206656 | tf_op jit(solution)/shard_map/pbckyz,pqkn->qbcnyz/dot_general | solution.py:80
  280.5 11.4 %copy.121 = f32[2,1,3,192,6,192]{5,0,4,2,1,3:T(2,128)} copy(f32[2,1,3,192,6,192]{5,3,4,2,0,1:T(8,128)} %fusion.14) | data formatting | bytes 10616832 | tf_op jit(solution)/shard_map/pbckyz,pqkn->qbcnyz/transpose | solution.py:80
  291.9 4.3 all-to-all-start.3
  296.3 3.7 pad_maximum_fusion.1
  300.5 1.9 multiply_reduce_fusion.2
  306.3 1.8 collective-permute-start.6
  308.1 37.7 %collective-permute-done.6 = f32[2,1,1]{0,2,1:T(1,128)S(1)} collective-permute-done((f32[2,1,1]{0,2,1:T(1,128)S(1)}, f32[2,1,1]{0,2,1:T(1,128)S(1)}, u32[]{:S(2)}, u32[]{:S(2)}) %collective-permute-start.6) | collective-permute-done | bytes 40 | tf_op jit(solution)/shard_map/ppermute | solution.py:204
  345.9 3.5 collective-permute-done.7
  349.4 63.0 %collective-permute-done.8 = f32[2,1,1]{0,2,1:T(1,128)S(1)} collective-permute-done((f32[2,1,1]{0,2,1:T(1,128)S(1)}, f32[2,1,1]{0,2,1:T(1,128)S(1)}, u32[]{:S(2)}, u32[]{:S(2)}) %collective-permute-start.8) | collective-permute-done | bytes 40 | tf_op jit(solution)/shard_map/ppermute | solution.py:204
  412.4 3.9 collective-permute-start.9
  416.3 37.2 %collective-permute-done.9 = f32[2,1,1]{0,2,1:T(1,128)S(1)} collective-permute-done((f32[2,1,1]{0,2,1:T(1,128)S(1)}, f32[2,1,1]{0,2,1:T(1,128)S(1)}, u32[]{:S(2)}, u32[]{:S(2)}) %collective-permute-start.9) | collective-permute-done | bytes 40 | tf_op jit(solution)/shard_map/ppermute | solution.py:204
  456.0 8.4 %copy.122 = f32[2,1,3,192,6,192]{5,0,4,3,2,1:T(2,128)} copy(f32[2,1,3,192,6,192]{5,0,4,2,1,3:T(2,128)} %all-to-all-done.3) | data formatting | bytes 10616832 | tf_op jit(solution)/shard_map/all_to_all | solution.py:292
  464.4 9.3 %copy.123 = f32[2,1,3,6,32,6,192]{6,0,5,4,3,2,1:T(2,128)} copy(f32[2,1,3,6,32,6,192]{6,0,5,3,4,2,1:T(2,128)} %bitcast.240) | data formatting | bytes 10616832 | tf_op jit(solution)/shard_map/all_to_all | solution.py:292
  473.8 9.3 %fusion.17 = f32[2,3,6,192,192]{4,3,2,1,0:T(8,128)S(1)} fusion(f32[2,3,6,192,192]{4,0,3,2,1:T(2,128)} %bitcast.239, f32[1,2,192,192]{2,3,1,0:T(8,128)S(1)} %copy-done.6, f32[1,2,192,192]{2,3,1,0:T(8,128)S(1)} %get-tuple-element.33), kind=kOutput, calls=%fused_computation.30 | convolution fusion | flops 3057795072 | bytes 11206656 | tf_op jit(solution)/shard_map/pbcxkz,pqkn->qbcxnz/dot_general | solution.py:82
  483.0 6.1 %fusion.4 = f32[2,192,3,6,192,1]{4,1,5,3,2,0:T(8,128)S(1)} fusion(f32[2,3,6,192,192]{4,3,2,1,0:T(8,128)S(1)} %fusion.17, f32[1,2,192,192]{2,3,1,0:T(8,128)S(1)} %copy-done.6, f32[1,2,192,192]{2,3,1,0:T(8,128)S(1)} %get-tuple-element.33), kind=kOutput, calls=%fused_computation.6 | convolution fusion | flops 3057795072 | bytes 11206656 | tf_op jit(solution)/shard_map/pbcxyk,pqkn->qbcxyn/dot_general | solution.py:83
  492.9 3.7 copy.129
  (98 shorter events, 21.1 us)
Async XLA Ops:
  0.6 20.2 %copy-start = (bf16[1,2,3,6,192,192]{5,4,3,2,1,0:T(8,128)(2,1)S(1)}, bf16[1,2,3,6,192,192]{5,4,3,2,1,0:T(8,128)(2,1)}, u32[]{:S(2)}) copy-start(bf16[1,2,3,6,192,192]{5,4,3,2,1,0:T(8,128)(2,1)} %trial_ref.5) | copy-start | bytes 7962628
  41.8 1.3 collective-permute-start
  43.1 4.5 collective-permute-start.1
  47.6 3.7 collective-permute-start.2
  51.3 3.7 collective-permute-start.3
  55.0 4.7 collective-permute-start.4
  82.2 60.9 %all-to-all-start = ((f32[2,1,1,6,192,192]{5,0,3,2,1,4:T(2,128)}), f32[2,1,1,6,192,192]{5,0,3,2,1,4:T(2,128)S(1)}, u32[]{:S(2)}, u32[]{:S(2)}) async-start(f32[2,1,1,6,192,192]{5,0,3,2,1,4:T(2,128)} %copy.107), calls=%async_computation | async-start | bytes 4718592 | tf_op jit(solution)/shard_map/all_to_all | solution.py:289
  143.2 58.6 %all-to-all-start.1 = ((f32[2,1,1,6,192,192]{5,0,3,2,1,4:T(2,128)}), f32[2,1,1,6,192,192]{5,0,3,2,1,4:T(2,128)}, u32[]{:S(2)}, u32[]{:S(2)}) async-start(f32[2,1,1,6,192,192]{5,0,3,2,1,4:T(2,128)} %copy.111), calls=%async_computation.1 | async-start | bytes 4718592 | tf_op jit(solution)/shard_map/all_to_all | solution.py:289
  201.8 58.7 %all-to-all-start.2 = ((f32[2,1,1,6,192,192]{5,0,3,2,1,4:T(2,128)}), f32[2,1,1,6,192,192]{5,0,3,2,1,4:T(2,128)}, u32[]{:S(2)}, u32[]{:S(2)}) async-start(f32[2,1,1,6,192,192]{5,0,3,2,1,4:T(2,128)} %copy.115), calls=%async_computation.2 | async-start | bytes 4718592 | tf_op jit(solution)/shard_map/all_to_all | solution.py:289
  206.3 2.5 copy-start.4
  208.9 13.3 %copy-start.7 = (f32[1,2,192,192]{2,3,0,1:T(8,128)}, f32[1,2,192,192]{2,3,0,1:T(8,128)S(1)}, u32[]{:S(2)}) copy-start(f32[1,2,192,192]{2,3,0,1:T(8,128)S(1)} %get-tuple-element.34) | copy-start | bytes 884740
  208.9 13.3 %copy-start.9 = (f32[1,2,192,192]{2,3,0,1:T(8,128)}, f32[1,2,192,192]{2,3,0,1:T(8,128)S(1)}, u32[]{:S(2)}) copy-start(f32[1,2,192,192]{2,3,0,1:T(8,128)S(1)} %get-tuple-element.35) | copy-start | bytes 884740
  208.9 63.3 %copy-start.5 = (f32[1,2,192,192]{2,3,1,0:T(8,128)}, f32[1,2,192,192]{2,3,1,0:T(8,128)S(1)}, u32[]{:S(2)}) copy-start(f32[1,2,192,192]{2,3,1,0:T(8,128)S(1)} %get-tuple-element.36) | copy-start | bytes 884740
  208.9 3.7 copy-start.17
  222.2 44.3 %copy-start.1 = (f32[2,192,6,192,1]{3,1,4,2,0:T(8,128)}, f32[2,192,6,192,1]{3,1,4,2,0:T(8,128)S(1)}, u32[]{:S(2)}) copy-start(f32[2,192,6,192,1]{3,1,4,2,0:T(8,128)S(1)} %fusion.33) | copy-start | bytes 5308420
  263.1 1.0 copy-start.8
  263.1 1.1 copy-start.10
  263.1 3.4 copy-start.13
  263.1 3.4 copy-start.14
  263.1 3.4 copy-start.15
  263.1 3.4 copy-start.16
  264.2 2.4 copy-start.2
  264.2 2.7 copy-start.11
  264.2 3.0 copy-start.12
  266.5 2.2 copy-start.3
  291.9 8.1 %slice-start = ((s8[7077888]{0:T(1024)(128)(4,1)}), s8[2883584]{0:T(1024)(128)(4,1)S(1)}, s32[]{:S(2)}) async-start(s8[7077888]{0:T(1024)(128)(4,1)} %bitcast.241), calls=%async_computation.4 | async-start | bytes 5767168
  291.9 164.2 %all-to-all-start.3 = ((f32[2,1,3,192,6,192]{5,0,4,2,1,3:T(2,128)}), f32[2,1,3,192,6,192]{5,0,4,2,1,3:T(2,128)}, u32[]{:S(2)}, u32[]{:S(2)}) async-start(f32[2,1,3,192,6,192]{5,0,4,2,1,3:T(2,128)} %copy.121), calls=%async_computation.3 | async-start | bytes 14155776 | tf_op jit(solution)/shard_map/all_to_all | solution.py:292
  296.3 4.3 slice-start.1
  305.0 1.2 collective-permute-start.5
  306.3 39.5 %collective-permute-start.6 = (f32[2,1,1]{0,2,1:T(1,128)S(1)}, f32[2,1,1]{0,2,1:T(1,128)S(1)}, u32[]{:S(2)}, u32[]{:S(2)}) collective-permute-start(f32[2,1,1]{0,2,1:T(1,128)S(1)} %fusion.82), channel_id=1, source_target_pairs={{0,2},{1,3},{2,0},{3,1},{4,6},{5,7},{6,4},{7,5},{8,10},{9,11},{10,... | collective-permute-start | bytes 32 | tf_op jit(solution)/shard_map/ppermute | solution.py:204
  345.9 3.5 collective-permute-start.7
  349.4 63.0 %collective-permute-start.8 = (f32[2,1,1]{0,2,1:T(1,128)S(1)}, f32[2,1,1]{0,2,1:T(1,128)S(1)}, u32[]{:S(2)}, u32[]{:S(2)}) collective-permute-start(f32[2,1,1]{0,2,1:T(1,128)S(1)} %add.190), channel_id=1, source_target_pairs={{0,8},{1,9},{2,10},{3,11},{4,12},{5,13},{6,14},{7,15},{8,0},{9,1},... | collective-permute-start | bytes 32 | tf_op jit(solution)/shard_map/ppermute | solution.py:204
  412.4 41.2 %collective-permute-start.9 = (f32[2,1,1]{0,2,1:T(1,128)S(1)}, f32[2,1,1]{0,2,1:T(1,128)S(1)}, u32[]{:S(2)}, u32[]{:S(2)}) collective-permute-start(f32[2,1,1]{0,2,1:T(1,128)S(1)} %add.191), channel_id=1, source_target_pairs={{0,16},{1,17},{2,18},{3,19},{4,20},{5,21},{6,22},{7,23},{8,24},{9,... | collective-permute-start | bytes 32 | tf_op jit(solution)/shard_map/ppermute | solution.py:204
  464.4 9.4 %copy-start.6 = (f32[1,2,192,192]{2,3,1,0:T(8,128)S(1)}, f32[1,2,192,192]{2,3,1,0:T(8,128)}, u32[]{:S(2)}) copy-start(f32[1,2,192,192]{2,3,1,0:T(8,128)} %copy-done.5) | copy-start | bytes 884740
  489.5 0.7 copy-start.18

commit v7 on v5

--- a/solution.py
+++ b/solution.py
@@ -288,11 +288,28 @@
     wave_full = signed_wave(full_axis, grid_len)
     waves = (wave_x, wave_full, wave_full)
 
+    def exchange_rows(field, split_dim, keep_dim):
+        parts, bands, comps = field.shape[0], field.shape[1], field.shape[2]
+        order = (split_dim, 1, 2, keep_dim, 0, 5)
+        moved = jnp.transpose(field, order).reshape(wide_count, -1)
+        moved = lax.all_to_all(moved, "wide", split_axis=0, concat_axis=0, tiled=True)
+        local_split = field.shape[split_dim] // wide_count
+        moved = moved.reshape(
+            wide_count, local_split, bands, comps, field.shape[keep_dim], parts, field.shape[5]
+        )
+        return moved
+
     def send_out_one(field):
-        return lax.all_to_all(field, "wide", split_axis=4, concat_axis=3, tiled=True)
+        moved = exchange_rows(field, 4, 3)
+        moved = jnp.transpose(moved, (5, 2, 3, 0, 4, 1, 6))
+        shape = moved.shape
+        return moved.reshape(shape[0], shape[1], shape[2], shape[3] * shape[4], shape[5], shape[6])
 
     def send_home_one(field):
-        return lax.all_to_all(field, "wide", split_axis=3, concat_axis=4, tiled=True)
+        moved = exchange_rows(field, 3, 4)
+        moved = jnp.transpose(moved, (5, 2, 3, 1, 0, 4, 6))
+        shape = moved.shape
+        return moved.reshape(shape[0], shape[1], shape[2], shape[3], shape[4] * shape[5], shape[6])
 
     chunks = [front_pass((comp,), coef.T, wave_x, trial_bands, locked_bands) for comp in range(3)]
     results = [maxwell_pass(chunks, waves, inv_diag, inv_corr, send_out_one, send_home_one)]

time: 490 us -> 464 us (0.947)
  waiting for transfers between devices: 244 us -> 129 us
  local copies, waits for them, and re-layouts: 71.5 us -> 121 us
  other arithmetic: 19 us -> 61 us
    all_to_all x6, waiting for transfers between devices: 203 us -> 100 us  [exchange_rows(): lax.all_to_all(moved, 'wide', split_axis=0, concat_axis=0, tiled=True)]
    all_to_all x0 -> x6, other arithmetic: none -> 41.6 us  [exchange_rows(): lax.all_to_all(moved, 'wide', split_axis=0, concat_axis=0, tiled=True)]
    reshape x0 -> x6, local copies, waits for them, and re-layouts: none -> 26.1 us  [exchange_rows(): moved.reshape(wide_count, local_split, bands, comps, field.shape[keep_dim...]
    transpose x3 -> x12, local copies, waits for them, and re-layouts: 9.73 us -> 31.3 us  [the longest x6 20.1 us: exchange_rows(): moved = jnp.transpose(field, order).reshape(wide_count, -1)]
    all_to_all x9 -> x6, local copies, waits for them, and re-layouts: 15.9 us -> 31.8 us  [exchange_rows(): lax.all_to_all(moved, 'wide', split_axis=0, concat_axis=0, tiled=True)]
    pallas_call x3 -> x0, local copies, waits for them, and re-layouts: 14.8 us -> none  [front_pass(): pl.pallas_call(functools.partial(front_kernel, comps), grid=(band_count,...]
    ppermute x10, waiting for transfers between devices: 41.4 us -> 28.9 us  [butterfly_sum(): values = values + lax.ppermute(values, axis, pairs)]
    unnamed x34 -> x30, local copies, waits for them, and re-layouts: 13.7 us -> 14.1 us
  transfers between devices with their start and end apart: 16 -> 16, of which waited for: 15 -> 15; matrix products, arithmetic and copies ran while one was open for 13% -> 22% of each run, Pallas kernels for 5% -> 6%
where the time goes in v7:
time: 464 us; the launch traced here: 458 us
  waiting for transfers between devices  129 us (28%)
  local copies, waits for them, and re-layouts  121 us (26%)
  other arithmetic  61 us (13%)
  matrix products  54.2 us (12%)
  starting transfers between devices  49 us (11%)
  Pallas kernels  39 us (8%)
  between operations  5.23 us (1%)
    all_to_all x6, waiting for transfers between devices, exchange_rows(): lax.all_to_all(moved, 'wide', split_axis=0, concat_axis=0, tiled=True)  100 us
    all_to_all x6, other arithmetic, exchange_rows(): lax.all_to_all(moved, 'wide', split_axis=0, concat_axis=0, tiled=True)  41.6 us
    pallas_call x3, Pallas kernels, front_pass(): pl.pallas_call(functools.partial(front_kernel, comps), grid=(band_count,...  39 us
    all_to_all x6, local copies, waits for them, and re-layouts, exchange_rows(): lax.all_to_all(moved, 'wide', split_axis=0, concat_axis=0, tiled=True)  31.8 us
    ppermute x10, waiting for transfers between devices, butterfly_sum(): values = values + lax.ppermute(values, axis, pairs)  28.9 us
    all_to_all x6, starting transfers between devices, exchange_rows(): lax.all_to_all(moved, 'wide', split_axis=0, concat_axis=0, tiled=True)  28.9 us
    reshape x6, local copies, waits for them, and re-layouts, exchange_rows(): moved.reshape(wide_count, local_split, bands, comps, field.shape[keep_dim...  26.1 us
    dot_general x6, matrix products, transform(): jnp.einsum('pbckyz,pqkn->qbcnyz', stacked, table, precision=three_pass)  22.6 us
  transfers between devices with their start and end apart: 16, of which 15 were waited for; matrix products, arithmetic and copies ran while one was open for 22% of the time, Pallas kernels for 6%

profile of v7, /device:TPU:0, one launch (start us, length us, event | category | flops | bytes accessed | tf_op | source)
XLA Modules:
  0.0 458.5 jit_solution(2057159393306376825)
XLA Ops:
  0.6 5.7 %copy.285 = bf16[1,2,3,6,192,192]{5,1,4,3,2,0:T(2,128)(2,1)S(1)} copy(bf16[1,2,3,6,192,192]{5,4,3,2,1,0:T(8,128)(2,1)} %trial_ref.5) | data formatting | bytes 5308416 | tf_op args[0]
  6.3 13.8 %copy.183 = bf16[8,3,6,192,192]{4,0,3,2,1:T(8,128)(2,1)S(1)} copy(bf16[8,3,6,192,192]{4,3,2,1,0:T(8,128)(2,1)} %bitcast.340) | data formatting | bytes 21233664 | tf_op jit(solution)/shard_map/reshape | solution.py:271
  20.1 16.5 %fusion.75 = f32[10,10]{0,1:T(8,128)S(1)} fusion(bf16[2,3,6,192,192]{4,0,3,2,1:T(2,128)(2,1)S(1)} %bitcast.362, bf16[8,3,6,192,192]{4,0,3,2,1:T(8,128)(2,1)S(1)} %copy.183), kind=kOutput, calls=%fused_computation.95 | convolution fusion | flops 159252480 | bytes 13271440 | tf_op jit(solution)/shard_map/icxyz,jcxyz->ij/dot_general | solution.py:275
  59.1 12.9 %shard_map.168 = f32[2,1,1,6,192,192]{5,4,3,2,1,0:T(8,128)} custom-call(f32[1,8]{1,0:T(1,128)} %fusion.104.coef_ref, f32[6]{0:T(128)} %fusion.112.qx_ref, bf16[1,2,3,6,192,192]{5,4,3,2,1,0:T(8,128)(2,1)} %trial_ref.5, bf16[4,2,3,6,192,192]{5,4,3,2,1,0:T(8,128)(2,1)} %locked_ref.5, bf16[192,192]{1,0:T(8,128)(2,1)} %constant.128.clone.chi_ref, ...), custom_call_target="tpu_custom_call" | custom-call | tf_op jit(solution)/shard_map/pallas_call | solution.py:180
  72.0 3.5 copy.101
  75.5 4.7 %all_to_all.49 = f32[32,1,13824]{2,1,0:T(1,128)} reshape(f32[192,1,1,6,2,192]{5,4,3,0,2,1:T(2,128)S(1)} %copy.101) | data formatting | bytes 3538944 | tf_op jit(solution)/shard_map/all_to_all | solution.py:295
  80.3 6.5 %all-to-all-start.1 = ((f32[32,1,13824]{2,1,0:T(1,128)}), f32[32,1,13824]{2,1,0:T(1,128)}, u32[]{:S(2)}, u32[]{:S(2)}) async-start(f32[32,1,13824]{2,1,0:T(1,128)} %all_to_all.49), calls=%async_computation.1 | async-start | bytes 3538944 | tf_op jit(solution)/shard_map/all_to_all | solution.py:295
  86.8 13.0 %shard_map.167 = f32[2,1,1,6,192,192]{5,4,3,2,1,0:T(8,128)} custom-call(f32[1,8]{1,0:T(1,128)} %fusion.104.coef_ref, f32[6]{0:T(128)} %fusion.112.qx_ref, bf16[1,2,3,6,192,192]{5,4,3,2,1,0:T(8,128)(2,1)} %trial_ref.5, bf16[4,2,3,6,192,192]{5,4,3,2,1,0:T(8,128)(2,1)} %locked_ref.5, bf16[192,192]{1,0:T(8,128)(2,1)} %constant.128.clone.chi_ref, ...), custom_call_target="tpu_custom_call" | custom-call | tf_op jit(solution)/shard_map/pallas_call | solution.py:180
  99.8 3.5 copy.97
  103.3 4.7 %all_to_all.48 = f32[32,1,13824]{2,1,0:T(1,128)} reshape(f32[192,1,1,6,2,192]{5,4,3,0,2,1:T(2,128)S(1)} %copy.97) | data formatting | bytes 3538944 | tf_op jit(solution)/shard_map/all_to_all | solution.py:295
  108.0 20.6 %all-to-all-done.1 = f32[32,1,13824]{2,1,0:T(1,128)} async-done(((f32[32,1,13824]{2,1,0:T(1,128)}), f32[32,1,13824]{2,1,0:T(1,128)}, u32[]{:S(2)}, u32[]{:S(2)}) %all-to-all-start.1) | async-done | bytes 1769504 | tf_op jit(solution)/shard_map/all_to_all | solution.py:295
  128.6 4.1 all-to-all-start
  132.7 13.1 %shard_map.169 = f32[2,1,1,6,192,192]{5,4,3,2,1,0:T(8,128)} custom-call(f32[1,8]{1,0:T(1,128)} %fusion.104.coef_ref, f32[6]{0:T(128)} %fusion.112.qx_ref, bf16[1,2,3,6,192,192]{5,4,3,2,1,0:T(8,128)(2,1)} %trial_ref.5, bf16[4,2,3,6,192,192]{5,4,3,2,1,0:T(8,128)(2,1)} %locked_ref.5, bf16[192,192]{1,0:T(8,128)(2,1)} %constant.128.clone.chi_ref, ...), custom_call_target="tpu_custom_call" | custom-call | tf_op jit(solution)/shard_map/pallas_call | solution.py:180
  145.8 3.5 copy.105
  149.2 4.7 %all_to_all.50 = f32[32,1,13824]{2,1,0:T(1,128)} reshape(f32[192,1,1,6,2,192]{5,4,3,0,2,1:T(2,128)S(1)} %copy.105) | data formatting | bytes 3538944 | tf_op jit(solution)/shard_map/all_to_all | solution.py:295
  154.0 20.5 %all-to-all-done = f32[32,1,13824]{2,1,0:T(1,128)} async-done(((f32[32,1,13824]{2,1,0:T(1,128)}), f32[32,1,13824]{2,1,0:T(1,128)}, u32[]{:S(2)}, u32[]{:S(2)}) %all-to-all-start) | async-done | bytes 1769504 | tf_op jit(solution)/shard_map/all_to_all | solution.py:295
  174.5 4.5 all-to-all-start.2
  188.0 6.9 %reduce.14 = f32[32,13824]{1,0:T(8,128)} reduce(f32[32,1,13824]{2,1,0:T(1,128)} %all-to-all-done.1, f32[]{:T(128)} %constant.140), dimensions={1}, to_apply=%all_to_all.39.reduce_sub_computation | reduce | bytes 3538948 | tf_op jit(solution)/shard_map/all_to_all | solution.py:295
  194.9 4.0 reshape.605
  201.1 6.9 %reduce.13 = f32[32,13824]{1,0:T(8,128)} reduce(f32[32,1,13824]{2,1,0:T(1,128)} %all-to-all-done, f32[]{:T(128)} %constant.140), dimensions={1}, to_apply=%all_to_all.37.reduce_sub_computation | reduce | bytes 3538948 | tf_op jit(solution)/shard_map/all_to_all | solution.py:295
  208.0 4.1 reshape.603
  216.1 3.6 fusion.33
  220.8 6.9 %reduce.15 = f32[32,13824]{1,0:T(8,128)} reduce(f32[32,1,13824]{2,1,0:T(1,128)} %all-to-all-done.2, f32[]{:T(128)} %constant.140), dimensions={1}, to_apply=%all_to_all.41.reduce_sub_computation | reduce | bytes 3538948 | tf_op jit(solution)/shard_map/all_to_all | solution.py:295
  227.7 5.1 %reshape.607 = f32[32,6,1,1,6,2,192]{6,5,4,1,0,3,2:T(2,128)} reshape(f32[32,13824]{1,0:T(8,128)} %reduce.15) | data formatting | bytes 3538944 | tf_op jit(solution)/shard_map/reshape | solution.py:297
  235.6 7.1 %fusion.23 = (f32[2,192,6,192]{3,1,2,0:T(8,128)}, f32[2,192,6,192]{3,1,2,0:T(8,128)}, f32[2,192,6,192]{3,1,2,0:T(8,128)S(1)}, f32[2,192,6,192,1]{3,1,4,2,0:T(8,128)}) fusion(f32[2,192,6,192,1]{3,1,4,2,0:T(8,128)S(1)} %fusion.31, f32[2,192,6,192,1]{3,1,4,2,0:T(8,128)S(1)} %copy-done, f32[192,6,192]{2,0,1:T(8,128)} %get-tuple-element.21, ...), kind=kOutput, calls=%fused_computation.42 | convolution fusion | flops 1025998848 | bytes 18284544 | tf_op jit(solution)/shard_map/pbckyz,pqkn->qbcnyz/dot_general | solution.py:80
  245.0 3.2 copy.129
  248.2 6.0 %all_to_all.53 = f32[32,1,13824]{2,1,0:T(1,128)} reshape(f32[192,1,1,6,2,192]{5,4,3,0,2,1:T(2,128)} %copy.129) | data formatting | bytes 3538944 | tf_op jit(solution)/shard_map/all_to_all | solution.py:295
  254.2 4.9 %all-to-all-start.5 = ((f32[32,1,13824]{2,1,0:T(1,128)}), f32[32,1,13824]{2,1,0:T(1,128)}, u32[]{:S(2)}, u32[]{:S(2)}) async-start(f32[32,1,13824]{2,1,0:T(1,128)} %all_to_all.53), calls=%async_computation.5 | async-start | bytes 3538944 | tf_op jit(solution)/shard_map/all_to_all | solution.py:295
  259.1 3.7 fusion.57
  262.8 3.2 copy.120
  266.1 5.8 %all_to_all.52 = f32[32,1,13824]{2,1,0:T(1,128)} reshape(f32[192,1,1,6,2,192]{5,4,3,0,2,1:T(2,128)} %copy.120) | data formatting | bytes 3538944 | tf_op jit(solution)/shard_map/all_to_all | solution.py:295
  271.9 29.0 %all-to-all-done.5 = f32[32,1,13824]{2,1,0:T(1,128)} async-done(((f32[32,1,13824]{2,1,0:T(1,128)}), f32[32,1,13824]{2,1,0:T(1,128)}, u32[]{:S(2)}, u32[]{:S(2)}) %all-to-all-start.5) | async-done | bytes 1769504 | tf_op jit(solution)/shard_map/all_to_all | solution.py:295
  300.9 4.3 all-to-all-start.4
  305.2 3.7 fusion.48
  312.2 5.8 %all_to_all.51 = f32[32,1,13824]{2,1,0:T(1,128)} reshape(f32[192,1,1,6,2,192]{5,4,3,0,2,1:T(2,128)} %copy.111) | data formatting | bytes 3538944 | tf_op jit(solution)/shard_map/all_to_all | solution.py:295
  318.0 29.0 %all-to-all-done.4 = f32[32,1,13824]{2,1,0:T(1,128)} async-done(((f32[32,1,13824]{2,1,0:T(1,128)}), f32[32,1,13824]{2,1,0:T(1,128)}, u32[]{:S(2)}, u32[]{:S(2)}) %all-to-all-start.4) | async-done | bytes 1769504 | tf_op jit(solution)/shard_map/all_to_all | solution.py:295
  347.0 4.5 all-to-all-start.3
  371.7 9.7 %collective-permute-done.8 = f32[2,1,1]{0,2,1:T(1,128)S(1)} collective-permute-done((f32[2,1,1]{0,2,1:T(1,128)S(1)}, f32[2,1,1]{0,2,1:T(1,128)S(1)}, u32[]{:S(2)}, u32[]{:S(2)}) %collective-permute-start.8) | collective-permute-done | bytes 40 | tf_op jit(solution)/shard_map/ppermute | solution.py:204
  381.4 3.8 collective-permute-start.9
  385.2 8.2 %collective-permute-done.9 = f32[2,1,1]{0,2,1:T(1,128)S(1)} collective-permute-done((f32[2,1,1]{0,2,1:T(1,128)S(1)}, f32[2,1,1]{0,2,1:T(1,128)S(1)}, u32[]{:S(2)}, u32[]{:S(2)}) %collective-permute-start.9) | collective-permute-done | bytes 40 | tf_op jit(solution)/shard_map/ppermute | solution.py:204
  395.9 6.9 %reduce.18 = f32[32,13824]{1,0:T(8,128)} reduce(f32[32,1,13824]{2,1,0:T(1,128)} %all-to-all-done.5, f32[]{:T(128)} %constant.140), dimensions={1}, to_apply=%all_to_all.47.reduce_sub_computation | reduce | bytes 3538948 | tf_op jit(solution)/shard_map/all_to_all | solution.py:295
  402.7 4.0 reshape.615
  409.0 6.9 %reduce.17 = f32[32,13824]{1,0:T(8,128)} reduce(f32[32,1,13824]{2,1,0:T(1,128)} %all-to-all-done.4, f32[]{:T(128)} %constant.140), dimensions={1}, to_apply=%all_to_all.45.reduce_sub_computation | reduce | bytes 3538948 | tf_op jit(solution)/shard_map/all_to_all | solution.py:295
  415.9 4.1 reshape.612
  428.2 3.5 fusion.63
  431.7 7.1 %reduce.16 = f32[32,13824]{1,0:T(8,128)} reduce(f32[32,1,13824]{2,1,0:T(1,128)} %all-to-all-done.3, f32[]{:T(128)} %constant.140), dimensions={1}, to_apply=%all_to_all.43.reduce_sub_computation | reduce | bytes 3538948 | tf_op jit(solution)/shard_map/all_to_all | solution.py:295
  438.8 4.7 %reshape.609 = f32[32,6,1,1,6,2,192]{6,5,4,1,0,3,2:T(2,128)} reshape(f32[32,13824]{1,0:T(8,128)} %reduce.16) | data formatting | bytes 3538944 | tf_op jit(solution)/shard_map/reshape | solution.py:297
  454.5 3.7 copy.137
  (110 shorter events, 86.8 us)
Async XLA Ops:
  36.6 1.3 collective-permute-start
  38.0 4.5 collective-permute-start.1
  42.4 3.7 collective-permute-start.2
  46.1 3.7 collective-permute-start.3
  49.8 4.7 %collective-permute-start.4 = (f32[10,10]{0,1:T(8,128)S(1)}, f32[10,10]{0,1:T(8,128)S(1)}, u32[]{:S(2)}, u32[]{:S(2)}) collective-permute-start(f32[10,10]{0,1:T(8,128)S(1)} %add.184), channel_id=1, source_target_pairs={{0,16},{1,17},{2,18},{3,19},{4,20},{5,21},{6,22},{7,23},{8,24},{9,... | collective-permute-start | bytes 1208 | tf_op jit(solution)/shard_map/ppermute | solution.py:204
  80.3 48.3 %all-to-all-start.1 = ((f32[32,1,13824]{2,1,0:T(1,128)}), f32[32,1,13824]{2,1,0:T(1,128)}, u32[]{:S(2)}, u32[]{:S(2)}) async-start(f32[32,1,13824]{2,1,0:T(1,128)} %all_to_all.49), calls=%async_computation.1 | async-start | bytes 3538944 | tf_op jit(solution)/shard_map/all_to_all | solution.py:295
  128.6 45.9 %all-to-all-start = ((f32[32,1,13824]{2,1,0:T(1,128)}), f32[32,1,13824]{2,1,0:T(1,128)}, u32[]{:S(2)}, u32[]{:S(2)}) async-start(f32[32,1,13824]{2,1,0:T(1,128)} %all_to_all.48), calls=%async_computation | async-start | bytes 3538944 | tf_op jit(solution)/shard_map/all_to_all | solution.py:295
  174.5 46.3 %all-to-all-start.2 = ((f32[32,1,13824]{2,1,0:T(1,128)}), f32[32,1,13824]{2,1,0:T(1,128)}, u32[]{:S(2)}, u32[]{:S(2)}) async-start(f32[32,1,13824]{2,1,0:T(1,128)} %all_to_all.50), calls=%async_computation.2 | async-start | bytes 3538944 | tf_op jit(solution)/shard_map/all_to_all | solution.py:295
  179.0 3.3 copy-start.5
  182.3 3.3 copy-start.12
  212.1 1.7 copy-start.7
  212.1 1.7 copy-start.9
  232.8 2.6 copy-start
  232.8 2.6 copy-start.10
  232.8 2.8 copy-start.11
  242.7 2.3 copy-start.3
  254.2 46.7 %all-to-all-start.5 = ((f32[32,1,13824]{2,1,0:T(1,128)}), f32[32,1,13824]{2,1,0:T(1,128)}, u32[]{:S(2)}, u32[]{:S(2)}) async-start(f32[32,1,13824]{2,1,0:T(1,128)} %all_to_all.53), calls=%async_computation.5 | async-start | bytes 3538944 | tf_op jit(solution)/shard_map/all_to_all | solution.py:295
  300.9 46.1 %all-to-all-start.4 = ((f32[32,1,13824]{2,1,0:T(1,128)}), f32[32,1,13824]{2,1,0:T(1,128)}, u32[]{:S(2)}, u32[]{:S(2)}) async-start(f32[32,1,13824]{2,1,0:T(1,128)} %all_to_all.52), calls=%async_computation.4 | async-start | bytes 3538944 | tf_op jit(solution)/shard_map/all_to_all | solution.py:295
  347.0 84.6 %all-to-all-start.3 = ((f32[32,1,13824]{2,1,0:T(1,128)}), f32[32,1,13824]{2,1,0:T(1,128)}, u32[]{:S(2)}, u32[]{:S(2)}) async-start(f32[32,1,13824]{2,1,0:T(1,128)} %all_to_all.51), calls=%async_computation.3 | async-start | bytes 3538944 | tf_op jit(solution)/shard_map/all_to_all | solution.py:295
  351.6 3.1 copy-start.1
  351.6 3.8 copy-start.2
  351.6 4.5 copy-start.4
  361.5 1.2 collective-permute-start.5
  362.7 3.5 collective-permute-start.6
  366.4 3.5 collective-permute-start.7
  369.9 11.5 %collective-permute-start.8 = (f32[2,1,1]{0,2,1:T(1,128)S(1)}, f32[2,1,1]{0,2,1:T(1,128)S(1)}, u32[]{:S(2)}, u32[]{:S(2)}) collective-permute-start(f32[2,1,1]{0,2,1:T(1,128)S(1)} %add.202), channel_id=1, source_target_pairs={{0,8},{1,9},{2,10},{3,11},{4,12},{5,13},{6,14},{7,15},{8,0},{9,1},... | collective-permute-start | bytes 32 | tf_op jit(solution)/shard_map/ppermute | solution.py:204
  381.4 12.0 %collective-permute-start.9 = (f32[2,1,1]{0,2,1:T(1,128)S(1)}, f32[2,1,1]{0,2,1:T(1,128)S(1)}, u32[]{:S(2)}, u32[]{:S(2)}) collective-permute-start(f32[2,1,1]{0,2,1:T(1,128)S(1)} %add.203), channel_id=1, source_target_pairs={{0,16},{1,17},{2,18},{3,19},{4,20},{5,21},{6,22},{7,23},{8,24},{9,... | collective-permute-start | bytes 32 | tf_op jit(solution)/shard_map/ppermute | solution.py:204
  420.0 1.7 copy-start.8
  448.2 2.1 copy-start.6
  450.9 0.8 copy-start.13
